TPU v7x, 256 devices: a whole 4x4x8 slice. The times are simulated.
256 devices in a mesh: grp: 4 (over y), mdl: 64 (over z, x, core).
Axes of the slice: x: 4, y: 4, z: 8, core: 2. Of those that a mesh axis runs over, the one named last changes fastest.
Arguments:
- pol_hidden: bfloat16 [1024, 4096], P(('grp', 'mdl')), may hold values from -6 to 6
- ref_hidden: bfloat16 [1024, 4096], P(('grp', 'mdl')), may hold values from -6 to 6
- pol_mlp_gain: bfloat16 [4096], replicated, may hold values from 0.099609375 to 1.8984375
- ref_mlp_gain: bfloat16 [4096], replicated, may hold values from 0.099609375 to 1.8984375
- pol_final_gain: bfloat16 [4096], replicated, may hold values from 0.099609375 to 1.8984375
- ref_final_gain: bfloat16 [4096], replicated, may hold values from 0.099609375 to 1.8984375
- pol_gate: bfloat16 [4096, 11008], P(None, 'mdl'), may hold values from -0.09375 to 0.09375
- pol_up: bfloat16 [4096, 11008], P(None, 'mdl'), may hold values from -0.09375 to 0.09375
- pol_down: bfloat16 [11008, 4096], P('mdl'), may hold values from -0.109375 to 0.109375
- ref_gate: bfloat16 [4096, 11008], P(None, 'mdl'), may hold values from -0.09375 to 0.09375
- ref_up: bfloat16 [4096, 11008], P(None, 'mdl'), may hold values from -0.09375 to 0.09375
- ref_down: bfloat16 [11008, 4096], P('mdl'), may hold values from -0.109375 to 0.109375
- pol_head: bfloat16 [64000, 4096], P(('grp', 'mdl')), may hold values from -20 to 20
- ref_head: bfloat16 [64000, 4096], P(('grp', 'mdl')), may hold values from -20 to 20
- token_ids: int32 [1024], replicated, may hold values from 0 to 63999
- lengths: int32 [16], replicated, may hold values from 1 to 160, 1024 in all
Outputs:
- pol_out: bfloat16 [1024, 4096], P(('grp', 'mdl'))
- ref_out: bfloat16 [1024, 4096], P(('grp', 'mdl'))
- rollout_ratio: float32 [16], replicated
Inputs may be any that keep to these rules, and one draw needn't show every extreme that they name: Rollout lengths sum to 1024; the longest is exactly 160.
All inputs are finite; a program needn't handle non-finite values.
Results may differ from a plain program's by a relative error of at most 0.012.
The roundings to bfloat16 on the way count: a program that leaves them out, or rounds other values in their place, can miss the bound.
Values may be sent and summed in bfloat16 or wider, within the bound.
No kernel may reach another device: no remote copies, remote signals or barrier semaphores. Data moves between devices by JAX's collectives and lax.ppermute only.
A program may use at most 128 MiB of HBM per device.

v0:
```python
import jax
import jax.numpy as jnp
from jax import lax
from jax.sharding import PartitionSpec as P


def rms_rows(rows, gain):
    values = rows.astype(jnp.float32)
    scale = lax.rsqrt(jnp.mean(values * values, axis=-1, keepdims=True) + 1e-05)
    return (values * scale * gain.astype(jnp.float32)).astype(jnp.bfloat16)


def mlp_hidden(piece, gain, w_gate, w_up):
    normed = rms_rows(piece, gain)
    gate = jnp.dot(normed, w_gate, preferred_element_type=jnp.float32)
    upper = jnp.dot(normed, w_up, preferred_element_type=jnp.float32)
    return (jax.nn.silu(gate) * upper).astype(jnp.bfloat16)


def vocab_terms(token_rows, head_rows, targets, vocab):
    logits = jnp.einsum("td,vd->tv", token_rows, head_rows, preferred_element_type=jnp.float32)
    peak = jnp.max(logits, axis=1)
    total = jnp.sum(jnp.exp(logits - peak[:, None]), axis=1)
    target = jnp.sum(jnp.where(targets[:, None] == vocab[None, :], logits, 0.0), axis=1)
    return (peak, total, target)


def rollout_totals(log_ratio, positions, lengths):
    ends = jnp.cumsum(lengths)
    owner = jnp.sum((positions[:, None] >= ends[None, :]).astype(jnp.int32), axis=1)
    onehot = (owner[:, None] == jnp.arange(lengths.shape[0], dtype=jnp.int32)[None, :]).astype(
        jnp.float32
    )
    return jnp.sum(log_ratio[:, None] * onehot, axis=0)


def per_device(
    pol_hidden,
    ref_hidden,
    pol_mlp_gain,
    ref_mlp_gain,
    pol_final_gain,
    ref_final_gain,
    pol_gate,
    pol_up,
    pol_down,
    ref_gate,
    ref_up,
    ref_down,
    pol_head,
    ref_head,
    token_ids,
    lengths,
):
    results = []
    models = (
        (pol_hidden, pol_mlp_gain, pol_gate, pol_up, pol_down),
        (ref_hidden, ref_mlp_gain, ref_gate, ref_up, ref_down),
    )
    for hidden_in, gain, w_gate, w_up, w_down in models:

        def expand(piece, start, gain=gain, w_gate=w_gate, w_up=w_up):
            return mlp_hidden(piece, gain, w_gate, w_up)

        hidden = expand(lax.all_gather(hidden_in, "mdl", axis=0, tiled=True), jnp.int32(0))

        def project(start, count, hidden=hidden, w_down=w_down):
            return jnp.dot(hidden, w_down, preferred_element_type=jnp.float32)

        mixed = lax.psum_scatter(
            project(jnp.int32(0), hidden_in.shape[0] * lax.axis_size("mdl")),
            "mdl",
            scatter_dimension=0,
            tiled=True,
        )
        results.append((hidden_in.astype(jnp.float32) + mixed).astype(jnp.bfloat16))
    finals = [rms_rows(results[0], pol_final_gain), rms_rows(results[1], ref_final_gain)]
    voc_dev = pol_head.shape[0]
    members = lax.axis_size("mdl")
    group = lax.axis_index("grp")
    member = lax.axis_index("mdl")
    pol_rows, ref_rows = (
        lax.all_gather(finals[0], ("grp", "mdl"), axis=0, tiled=True),
        lax.all_gather(finals[1], ("grp", "mdl"), axis=0, tiled=True),
    )
    positions = jnp.arange(pol_rows.shape[0], dtype=jnp.int32)
    vocab = (group * members + member) * voc_dev + jnp.arange(voc_dev, dtype=jnp.int32)
    pol_terms = vocab_terms(pol_rows, pol_head, token_ids, vocab)
    ref_terms = vocab_terms(ref_rows, ref_head, token_ids, vocab)
    peaks = lax.pmax((pol_terms[0], ref_terms[0]), ("grp", "mdl"))
    sums = lax.psum(
        (
            pol_terms[1] * jnp.exp(pol_terms[0] - peaks[0]),
            pol_terms[2],
            ref_terms[1] * jnp.exp(ref_terms[0] - peaks[1]),
            ref_terms[2],
        ),
        ("grp", "mdl"),
    )
    pol_logp = sums[1] - peaks[0] - jnp.log(sums[0])
    ref_logp = sums[3] - peaks[1] - jnp.log(sums[2])
    rollout_ratio = rollout_totals(pol_logp - ref_logp, positions, lengths)
    return (results[0], results[1], rollout_ratio)


def solution(mesh):
    placed = (
        P(("grp", "mdl"), None),
        P(("grp", "mdl"), None),
        P(),
        P(),
        P(),
        P(),
        P(None, "mdl"),
        P(None, "mdl"),
        P("mdl", None),
        P(None, "mdl"),
        P(None, "mdl"),
        P("mdl", None),
        P(("grp", "mdl"), None),
        P(("grp", "mdl"), None),
        P(),
        P(),
    )
    return jax.shard_map(
        per_device,
        mesh=mesh,
        in_specs=placed,
        out_specs=(P(("grp", "mdl"), None), P(("grp", "mdl"), None), P()),
        check_vma=False,
    )
```

profile of v0, /device:TPU:6, one launch (start us, length us, event | category | flops | bytes accessed | tf_op | source)
XLA Modules:
  0.0 818.3 jit_solution(5168596979703755205)
XLA Ops:
  8.0 0.7 all-gather.9.cloned.1.call-update
  8.7 1.3 convert_element_type.66
  10.0 0.7 convert_element_type.60
  10.7 79.3 %all-gather.11.cloned.1.call-done = bf16[64,4,4096]{2,1,0:T(4,128)(2,1)} async-done(((bf16[1,4,4096]{2,1,0:T(4,128)(2,1)}), bf16[64,4,4096]{2,1,0:T(4,128)(2,1)}) %all-gather.11.cloned.1.call-update) | async-done | bytes 2097168 | tf_op jit(solution)/shard_map/all_gather | solution.py:65
  90.0 4.3 reshape.86
  94.3 2.5 multiply_reduce_fusion
  97.4 70.3 %all-gather.9.cloned.1.call-done = bf16[64,4,4096]{2,1,0:T(4,128)(2,1)} async-done(((bf16[1,4,4096]{2,1,0:T(4,128)(2,1)}), bf16[64,4,4096]{2,1,0:T(4,128)(2,1)}) %all-gather.9.cloned.1.call-update) | async-done | bytes 2097168 | tf_op jit(solution)/shard_map/all_gather | solution.py:65
  167.7 4.2 reshape.85
  171.9 2.7 multiply_reduce_fusion.1
  175.4 3.1 fusion.31
  178.5 7.2 fusion.2
  185.7 4.4 fusion.30
  190.0 7.2 fusion.3
  199.2 201.1 %all-reduce.7.cloned.1.call-done = (f32[256,4096]{1,0:T(8,128)}, f32[256,4096]{1,0:T(8,128)}) async-done(((f32[256,4096]{1,0:T(8,128)}, f32[256,4096]{1,0:T(8,128)}), (f32[256,4096]{1,0:T(8,128)}, f32[256,4096]{1,0:T(8,128)})) %all-reduce.7.cloned.1.call-update) | async-done | bytes 8388624
  400.3 1.2 fusion.18
  403.5 118.5 %all-gather.15.cloned.1.call-done = bf16[256,4,4096]{2,1,0:T(4,128)(2,1)} async-done(((bf16[1,4,4096]{2,1,0:T(4,128)(2,1)}), bf16[256,4,4096]{2,1,0:T(4,128)(2,1)}) %all-gather.15.cloned.1.call-update) | async-done | bytes 8388624 | tf_op jit(solution)/shard_map/all_gather | solution.py:84
  522.0 12.5 %reshape.84 = bf16[1024,4096]{1,0:T(8,128)(2,1)} reshape(bf16[256,4,4096]{2,1,0:T(4,128)(2,1)} %all-gather.15.cloned.1.call-done) | data formatting | bytes 16777216
  534.6 5.8 fusion.35
  540.4 100.5 %all-gather.13.cloned.1.call-done = bf16[256,4,4096]{2,1,0:T(4,128)(2,1)} async-done(((bf16[1,4,4096]{2,1,0:T(4,128)(2,1)}), bf16[256,4,4096]{2,1,0:T(4,128)(2,1)}) %all-gather.13.cloned.1.call-update) | async-done | bytes 8388624 | tf_op jit(solution)/shard_map/all_gather | solution.py:83
  640.9 12.5 %reshape.82 = bf16[1024,4096]{1,0:T(8,128)(2,1)} reshape(bf16[256,4,4096]{2,1,0:T(4,128)(2,1)} %all-gather.13.cloned.1.call-done) | data formatting | bytes 16777216
  653.4 7.3 fusion.34
  660.8 74.8 %all-reduce.3 = (f32[1024]{0:T(1024)S(1)}, f32[1024]{0:T(1024)S(1)}) all-reduce(f32[1024]{0:T(1024)S(1)} %get-tuple-element.23, f32[1024]{0:T(1024)S(1)} %get-tuple-element.21), channel_id=1, replica_groups=mesh['grp'=4,'mdl'=64] {'grp','mdl'}, use_global_device_ids=true, to_apply=%region_17.18 | all-reduce | flops 2048 | bytes 16384 | tf_op jit(solution)/shard_map/pmax | solution.py:90
  735.6 1.7 fusion.4
  737.3 73.8 %all-reduce.2 = (f32[1024]{0:T(1024)S(1)}, f32[1024]{0:T(1024)S(1)}, f32[1024]{0:T(1024)S(1)}, f32[1024]{0:T(1024)S(1)}) all-reduce(f32[1024]{0:T(1024)S(1)} %exponential_multiply_fusion, f32[1024]{0:T(1024)S(1)} %get-tuple-element.8, f32[1024]{0:T(1024)S(1)} %exponential_multiply_fusion.1, ...), channel_id=1, replica_groups=mesh['grp'=4,'mdl'=64] {'grp','mdl'}, use_global_device_ids=true, to_apply=%region_19.20 | all-reduce | flops 4096 | bytes 32768 | tf_op jit(solution)/shard_map/psum | solution.py:91
  (53 shorter events, 6.0 us)
Async XLA Ops:
  7.2 527.4 %copy-start = (bf16[250,4096]{1,0:T(8,128)(2,1)S(1)}, bf16[250,4096]{1,0:T(8,128)(2,1)}, u32[]{:S(2)}) copy-start(bf16[250,4096]{1,0:T(8,128)(2,1)} %param.29) | copy-start | bytes 6144004
  7.2 82.8 %all-gather.11.cloned.1.call-start = ((), (), s32[]{:S(2)}) async-start(), calls=%async_computation.1 | async-start | bytes 2129920 | tf_op jit(solution)/shard_map/all_gather | solution.py:65
  7.9 159.8 %all-gather.9.cloned.1.call-start = ((), (), s32[]{:S(2)}) async-start(), calls=%async_computation | async-start | bytes 2129920 | tf_op jit(solution)/shard_map/all_gather | solution.py:65
  8.7 391.6 %all-reduce.7.cloned.1.call-start = ((), (), s32[]{:S(2)}) async-start(), calls=%async_computation.4 | async-start | bytes 16777216
  171.9 3.4 copy-start.1
  171.9 6.5 copy-start.2
  185.7 4.4 copy-start.3
  197.3 0.7 copy-start.8
  197.3 0.7 copy-start.12
  197.3 203.0 %copy-start.4 = (bf16[4,4096]{1,0:T(4,128)(2,1)S(1)}, bf16[4,4096]{1,0:T(4,128)(2,1)}, u32[]{:S(2)}) copy-start(bf16[4,4096]{1,0:T(4,128)(2,1)} %param.17) | copy-start | bytes 98308
  197.3 203.0 %copy-start.5 = (bf16[4,4096]{1,0:T(4,128)(2,1)S(1)}, bf16[4,4096]{1,0:T(4,128)(2,1)}, u32[]{:S(2)}) copy-start(bf16[4,4096]{1,0:T(4,128)(2,1)} %param.16) | copy-start | bytes 98308
  197.3 205.1 %copy-start.9 = (bf16[4096]{0:T(1024)(128)(2,1)S(1)}, bf16[4096]{0:T(1024)(128)(2,1)}, u32[]{:S(2)}) copy-start(bf16[4096]{0:T(1024)(128)(2,1)} %param.20) | copy-start | bytes 24580
  197.3 205.9 %copy-start.11 = (s32[16]{0:T(128)S(1)}, s32[16]{0:T(128)}, u32[]{:S(2)}) copy-start(s32[16]{0:T(128)} %param.31) | copy-start | bytes 196
  197.3 324.7 %all-gather.15.cloned.1.call-start = ((), (), s32[]{:S(2)}) async-start(), calls=%async_computation.3 | async-start | bytes 8421376 | tf_op jit(solution)/shard_map/all_gather | solution.py:84
  401.4 133.1 %copy-start.6 = (bf16[4,4096]{1,0:T(4,128)(2,1)}, bf16[4,4096]{1,0:T(4,128)(2,1)S(1)}, u32[]{:S(2)}) copy-start(bf16[4,4096]{1,0:T(4,128)(2,1)S(1)} %get-tuple-element.20) | copy-start | bytes 98308
  401.5 133.1 %copy-start.7 = (bf16[4,4096]{1,0:T(4,128)(2,1)}, bf16[4,4096]{1,0:T(4,128)(2,1)S(1)}, u32[]{:S(2)}) copy-start(bf16[4,4096]{1,0:T(4,128)(2,1)S(1)} %get-tuple-element.26) | copy-start | bytes 98308
  402.2 238.7 %all-gather.13.cloned.1.call-start = ((), (), s32[]{:S(2)}) async-start(), calls=%async_computation.2 | async-start | bytes 8421376 | tf_op jit(solution)/shard_map/all_gather | solution.py:83
  653.4 82.1 %copy-start.10 = (s32[1024]{0:T(1024)S(1)}, s32[1024]{0:T(1024)}, u32[]{:S(2)}) copy-start(s32[1024]{0:T(1024)} %param.30) | copy-start | bytes 12292
Sparse Core Ops, SparseCore 0:
  10.8 79.1 all-gather.10
  92.8 74.9 all-gather.8
  197.4 202.7 all-reduce.6
  404.3 117.7 all-gather.14
  526.0 114.8 all-gather.12
where the time goes:
time: 821 us; the launch traced here: 818 us
  waiting for transfers between devices  571 us (70%)
  blocking collectives  149 us (18%)
  local copies, waits for them, and re-layouts  35 us (4%)
  matrix products  35 us (4%)
  between operations  14.6 us (2%)
  other arithmetic  13.6 us (2%)
    unnamed x6, waiting for transfers between devices  202 us
    all_gather x2, waiting for transfers between devices, per_device(): lax.all_gather(hidden_in, 'mdl', axis=0, tiled=True)  150 us
    all_gather x1, waiting for transfers between devices, per_device(): lax.all_gather(finals[1], ('grp', 'mdl'), axis=0, tiled=True)  119 us
    all_gather x1, waiting for transfers between devices, per_device(): lax.all_gather(finals[0], ('grp', 'mdl'), axis=0, tiled=True)  101 us
    pmax x1, blocking collectives, per_device(): peaks = lax.pmax((pol_terms[0], ref_terms[0]), ('grp', 'mdl'))  74.8 us
    psum x1, blocking collectives, per_device(): lax.psum((pol_terms[1] * jnp.exp(pol_terms[0] - peaks[0]), pol_terms[2],...  73.8 us
    unnamed x29, local copies, waits for them, and re-layouts  26.4 us
  transfers between devices with their start and end apart: 5, of which 5 were waited for; matrix products, arithmetic and copies ran while one was open for 4% of the time, Pallas kernels for 0%

commit v1 on v0

v1 whole, which is shorter than its diff:
```python
import jax
import jax.numpy as jnp
from jax import lax
from jax.sharding import PartitionSpec as P


def rms_rows(rows, gain):
    values = rows.astype(jnp.float32)
    scale = lax.rsqrt(jnp.mean(values * values, axis=-1, keepdims=True) + 1e-05)
    return (values * scale * gain.astype(jnp.float32)).astype(jnp.bfloat16)


def mlp_partial(piece, gain, w_gate, w_up, w_down):
    normed = rms_rows(piece, gain)
    gate = jnp.dot(normed, w_gate, preferred_element_type=jnp.float32)
    upper = jnp.dot(normed, w_up, preferred_element_type=jnp.float32)
    hidden = (jax.nn.silu(gate) * upper).astype(jnp.bfloat16)
    return jnp.dot(hidden, w_down, preferred_element_type=jnp.float32)


def vocab_terms(token_rows, head_rows, targets, vocab):
    logits = jnp.einsum("td,vd->tv", token_rows, head_rows, preferred_element_type=jnp.float32)
    peak = jnp.max(logits, axis=1)
    total = jnp.sum(jnp.exp(logits - peak[:, None]), axis=1)
    target = jnp.sum(jnp.where(targets[:, None] == vocab[None, :], logits, 0.0), axis=1)
    return (peak, total, target)


def rollout_totals(log_ratio, positions, lengths):
    ends = jnp.cumsum(lengths)
    owner = jnp.sum((positions[:, None] >= ends[None, :]).astype(jnp.int32), axis=1)
    onehot = (owner[:, None] == jnp.arange(lengths.shape[0], dtype=jnp.int32)[None, :]).astype(
        jnp.float32
    )
    return jnp.sum(log_ratio[:, None] * onehot, axis=0)


def per_device(
    pol_hidden,
    ref_hidden,
    pol_mlp_gain,
    ref_mlp_gain,
    pol_final_gain,
    ref_final_gain,
    pol_gate,
    pol_up,
    pol_down,
    ref_gate,
    ref_up,
    ref_down,
    pol_head,
    ref_head,
    token_ids,
    lengths,
):
    rows = pol_hidden.shape[0]
    member = lax.axis_index("mdl")
    group = lax.axis_index("grp")
    members = lax.axis_size("mdl")
    both_in = lax.all_gather(jnp.stack([pol_hidden, ref_hidden]), "mdl", axis=1, tiled=True)
    partials = (
        mlp_partial(both_in[0], pol_mlp_gain, pol_gate, pol_up, pol_down),
        mlp_partial(both_in[1], ref_mlp_gain, ref_gate, ref_up, ref_down),
    )
    mixed = lax.psum(partials, "mdl")
    outs = [(both_in[i].astype(jnp.float32) + mixed[i]).astype(jnp.bfloat16) for i in range(2)]
    finals = jnp.stack([rms_rows(outs[0], pol_final_gain), rms_rows(outs[1], ref_final_gain)])
    own = [lax.dynamic_slice_in_dim(o, member * rows, rows, axis=0) for o in outs]
    every = lax.all_gather(finals, "grp", axis=1, tiled=True)
    voc_dev = pol_head.shape[0]
    positions = jnp.arange(every.shape[1], dtype=jnp.int32)
    vocab = (group * members + member) * voc_dev + jnp.arange(voc_dev, dtype=jnp.int32)
    pol_terms = vocab_terms(every[0], pol_head, token_ids, vocab)
    ref_terms = vocab_terms(every[1], ref_head, token_ids, vocab)
    peaks = lax.pmax(lax.pmax((pol_terms[0], ref_terms[0]), "mdl"), "grp")
    sums = lax.psum(
        lax.psum(
            (
                pol_terms[1] * jnp.exp(pol_terms[0] - peaks[0]),
                pol_terms[2],
                ref_terms[1] * jnp.exp(ref_terms[0] - peaks[1]),
                ref_terms[2],
            ),
            "mdl",
        ),
        "grp",
    )
    pol_logp = sums[1] - peaks[0] - jnp.log(sums[0])
    ref_logp = sums[3] - peaks[1] - jnp.log(sums[2])
    rollout_ratio = rollout_totals(pol_logp - ref_logp, positions, lengths)
    return (own[0], own[1], rollout_ratio)


def solution(mesh):
    placed = (
        P(("grp", "mdl"), None),
        P(("grp", "mdl"), None),
        P(),
        P(),
        P(),
        P(),
        P(None, "mdl"),
        P(None, "mdl"),
        P("mdl", None),
        P(None, "mdl"),
        P(None, "mdl"),
        P("mdl", None),
        P(("grp", "mdl"), None),
        P(("grp", "mdl"), None),
        P(),
        P(),
    )
    return jax.shard_map(
        per_device,
        mesh=mesh,
        in_specs=placed,
        out_specs=(P(("grp", "mdl"), None), P(("grp", "mdl"), None), P()),
        check_vma=False,
    )
```

time: 821 us -> 922 us (1.12); the launches traced: 818 us -> 908 us
  blocking collectives: 149 us -> 386 us
  waiting for transfers between devices: 571 us -> 435 us
  local copies, waits for them, and re-layouts: 35 us -> 23 us
    unnamed x6 -> x3, waiting for transfers between devices: 202 us -> 0.05 us
    psum x0 -> x1, waiting for transfers between devices: none -> 202 us  [per_device(): mixed = lax.psum(partials, 'mdl')]
    psum x1, blocking collectives: 73.8 us -> 246 us  [per_device(): lax.psum((pol_terms[1] * jnp.exp(pol_terms[0] - peaks[0]), pol_terms[2],...]
    all_gather x4 -> x2, waiting for transfers between devices: 369 us -> 233 us  [the longest x1 153 us: per_device(): every = lax.all_gather(finals, 'grp', axis=1, tiled=True)]
    pmax x1 -> x2, blocking collectives: 74.8 us -> 126 us  [per_device(): peaks = lax.pmax(lax.pmax((pol_terms[0], ref_terms[0]), 'mdl'), 'grp')]
    unnamed x29 -> x34, local copies, waits for them, and re-layouts: 26.4 us -> 6.11 us
    psum x0 -> x1, blocking collectives: none -> 14.4 us  [per_device(): lax.psum(lax.psum((pol_terms[1] * jnp.exp(pol_terms[0] - peaks[0]), pol_t...]
    slice x0 -> x1, local copies, waits for them, and re-layouts: none -> 13.2 us  [per_device(): both_in[i].astype(jnp.float32) + mixed[i]]
  transfers between devices with their start and end apart: 5 -> 3, of which waited for: 5 -> 3; matrix products, arithmetic and copies ran while one was open for 4% -> 1% of each run, Pallas kernels for 0% -> 0%
where the time goes in v1:
time: 922 us; the launch traced here: 908 us
  waiting for transfers between devices  435 us (47%)
  blocking collectives  386 us (42%)
  matrix products  27.8 us (3%)
  local copies, waits for them, and re-layouts  23 us (2%)
  other arithmetic  21.1 us (2%)
  between operations  13.9 us (2%)
    psum x1, blocking collectives, per_device(): lax.psum((pol_terms[1] * jnp.exp(pol_terms[0] - peaks[0]), pol_terms[2],...  246 us
    psum x1, waiting for transfers between devices, per_device(): mixed = lax.psum(partials, 'mdl')  202 us
    all_gather x1, waiting for transfers between devices, per_device(): every = lax.all_gather(finals, 'grp', axis=1, tiled=True)  153 us
    pmax x2, blocking collectives, per_device(): peaks = lax.pmax(lax.pmax((pol_terms[0], ref_terms[0]), 'mdl'), 'grp')  126 us
    all_gather x1, waiting for transfers between devices, per_device(): lax.all_gather(jnp.stack([pol_hidden, ref_hidden]), 'mdl', axis=1, tiled=...  80.3 us
  transfers between devices with their start and end apart: 3, of which 3 were waited for; matrix products, arithmetic and copies ran while one was open for 1% of the time, Pallas kernels for 0%

profile of v1, /device:TPU:6, one launch (start us, length us, event | category | flops | bytes accessed | tf_op | source)
XLA Modules:
  0.0 907.9 jit_solution(18328997950964783200)
XLA Ops:
  7.2 1.0 pad_maximum_fusion.1
  9.0 1.3 convert_element_type.62
  11.0 80.3 %all-gather.3.cloned.1.call-done = bf16[2,256,4096]{2,0,1:T(2,128)(2,1)} async-done(((bf16[2,4,4096]{2,0,1:T(2,128)(2,1)}), bf16[2,256,4096]{2,0,1:T(2,128)(2,1)}) %all-gather.3.cloned.1.call-update) | async-done | bytes 4194320 | tf_op jit(solution)/shard_map/all_gather | solution.py:60
  91.3 13.2 %fusion.48 = (bf16[1,256,4096]{2,0,1:T(2,128)(2,1)S(1)}, bf16[1,256,4096]{2,0,1:T(2,128)(2,1)S(1)}) fusion(bf16[2,256,4096]{2,0,1:T(2,128)(2,1)} %all-gather.3.cloned.1.call-done), kind=kLoop, calls=%fused_computation.76 | loop fusion | bytes 8388608 | tf_op jit(solution)/shard_map/slice | solution.py:66
  104.5 6.7 fusion.8
  112.5 1.6 fusion.30
  114.1 6.6 fusion.21
  120.7 3.7 fusion.26
  124.4 6.6 fusion.20
  131.7 202.2 %all-reduce.7.cloned.1.call-done = (f32[256,4096]{1,0:T(8,128)}, f32[256,4096]{1,0:T(8,128)}) async-done(((f32[256,4096]{1,0:T(8,128)}, f32[256,4096]{1,0:T(8,128)}), (f32[256,4096]{1,0:T(8,128)}, f32[256,4096]{1,0:T(8,128)})) %all-reduce.7.cloned.1.call-update) | async-done | bytes 8388624 | tf_op jit(solution)/shard_map/psum | solution.py:65
  333.9 3.8 fusion.2
  338.6 0.8 fusion.5
  341.5 2.3 pad_maximum_fusion
  344.7 1.5 constant_dynamic-slice_fusion.1
  346.2 1.5 constant_dynamic-slice_fusion
  347.7 152.7 %all-gather.5.cloned.1.call-done = bf16[2,1024,4096]{2,1,0:T(8,128)(2,1)} async-done(((bf16[2,256,4096]{2,1,0:T(8,128)(2,1)}), bf16[2,1024,4096]{2,1,0:T(8,128)(2,1)}) %all-gather.5.cloned.1.call-update) | async-done | bytes 16777232 | tf_op jit(solution)/shard_map/all_gather | solution.py:69
  500.4 5.9 fusion.49
  506.3 2.2 copy-done.14
  509.2 3.4 fusion.50
  512.6 116.1 %all-reduce.2 = (f32[1024]{0:T(1024)S(1)}, f32[1024]{0:T(1024)S(1)}) all-reduce(f32[1024]{0:T(1024)S(1)} %get-tuple-element.35, f32[1024]{0:T(1024)S(1)} %get-tuple-element.33), channel_id=1, replica_groups=mesh['grp'=4,'mdl'=64] {'mdl'}, use_global_device_ids=true, to_apply=%region_21.22 | all-reduce | flops 2048 | bytes 16384 | tf_op jit(solution)/shard_map/pmax | solution.py:75
  628.6 9.6 %all-reduce.4 = (f32[1024]{0:T(1024)S(1)}, f32[1024]{0:T(1024)S(1)}) all-reduce(f32[1024]{0:T(1024)S(1)} %get-tuple-element.15, f32[1024]{0:T(1024)S(1)} %get-tuple-element.16), channel_id=1, replica_groups=mesh['grp'=4,'mdl'=64] {'grp'}, use_global_device_ids=true, to_apply=%region_22.23 | all-reduce | flops 2048 | bytes 16384 | tf_op jit(solution)/shard_map/pmax | solution.py:75
  638.3 1.7 fusion.22
  640.0 246.3 %all-reduce = (f32[1024]{0:T(1024)S(1)}, f32[1024]{0:T(1024)S(1)}, f32[1024]{0:T(1024)S(1)}, f32[1024]{0:T(1024)S(1)}) all-reduce(f32[1024]{0:T(1024)S(1)} %exponential_multiply_fusion, f32[1024]{0:T(1024)S(1)} %get-tuple-element.8, f32[1024]{0:T(1024)S(1)} %exponential_multiply_fusion.1, ...), channel_id=1, replica_groups=mesh['grp'=4,'mdl'=64] {'mdl'}, use_global_device_ids=true, to_apply=%region_24.25 | all-reduce | flops 4096 | bytes 32768 | tf_op jit(solution)/shard_map/psum | solution.py:77
  886.3 14.4 %all-reduce.3 = (f32[1024]{0:T(1024)S(1)}, f32[1024]{0:T(1024)S(1)}, f32[1024]{0:T(1024)S(1)}, f32[1024]{0:T(1024)S(1)}) all-reduce(f32[1024]{0:T(1024)S(1)} %get-tuple-element.9, f32[1024]{0:T(1024)S(1)} %get-tuple-element.10, f32[1024]{0:T(1024)S(1)} %get-tuple-element.11, ...), channel_id=1, replica_groups=mesh['grp'=4,'mdl'=64] {'grp'}, use_global_device_ids=true, to_apply=%region_25.26 | all-reduce | flops 4096 | bytes 32768 | tf_op jit(solution)/shard_map/psum | solution.py:76
  (58 shorter events, 8.5 us)
Async XLA Ops:
  7.2 493.3 %copy-start = (bf16[250,4096]{1,0:T(8,128)(2,1)S(1)}, bf16[250,4096]{1,0:T(8,128)(2,1)}, u32[]{:S(2)}) copy-start(bf16[250,4096]{1,0:T(8,128)(2,1)} %param.28) | copy-start | bytes 6144004
  7.2 84.1 %all-gather.3.cloned.1.call-start = ((), (), s32[]{:S(2)}) async-start(), calls=%async_computation | async-start | bytes 4259840 | tf_op jit(solution)/shard_map/all_gather | solution.py:60
  8.9 325.0 %all-reduce.7.cloned.1.call-start = ((), (), s32[]{:S(2)}) async-start(), calls=%async_computation.2 | async-start | bytes 16777216 | tf_op jit(solution)/shard_map/psum | solution.py:65
  104.5 8.0 copy-start.8
  104.5 8.0 copy-start.16
  111.2 1.3 copy-start.2
  111.2 1.3 copy-start.12
  112.5 1.6 copy-start.6
  120.7 3.7 copy-start.7
  131.0 0.7 copy-start.9
  131.0 0.7 copy-start.10
  131.0 369.4 %all-gather.5.cloned.1.call-start = ((), (), s32[]{:S(2)}) async-start(), calls=%async_computation.1 | async-start | bytes 20971520 | tf_op jit(solution)/shard_map/all_gather | solution.py:69
  333.9 3.9 copy-start.1
  333.9 4.7 copy-start.5
  337.8 3.0 copy-start.3
  339.5 1.3 copy-start.4
  343.8 0.7 copy-start.13
  500.4 8.2 copy-start.14
  500.4 8.7 copy-start.15
  509.2 129.1 %copy-start.11 = (s32[1024]{0:T(1024)S(1)}, s32[1024]{0:T(1024)}, u32[]{:S(2)}) copy-start(s32[1024]{0:T(1024)} %param.30) | copy-start | bytes 12292
Sparse Core Ops, SparseCore 0:
  10.8 80.4 all-gather.2
  131.1 202.7 all-reduce.6
  343.9 156.4 all-gather.4

commit v2 on v1

--- a/solution.py
+++ b/solution.py
@@ -24,6 +24,12 @@
     total = jnp.sum(jnp.exp(logits - peak[:, None]), axis=1)
     target = jnp.sum(jnp.where(targets[:, None] == vocab[None, :], logits, 0.0), axis=1)
     return (peak, total, target)
+
+
+def merge_terms(lo, hi):
+    peak = jnp.maximum(lo[:, 0], hi[:, 0])
+    total = lo[:, 1] * jnp.exp(lo[:, 0] - peak) + hi[:, 1] * jnp.exp(hi[:, 0] - peak)
+    return jnp.stack([peak, total, lo[:, 2] + hi[:, 2]], axis=1)
 
 
 def rollout_totals(log_ratio, positions, lengths):
@@ -64,30 +70,34 @@
     )
     mixed = lax.psum(partials, "mdl")
     outs = [(both_in[i].astype(jnp.float32) + mixed[i]).astype(jnp.bfloat16) for i in range(2)]
-    finals = jnp.stack([rms_rows(outs[0], pol_final_gain), rms_rows(outs[1], ref_final_gain)])
+    finals = (rms_rows(outs[0], pol_final_gain), rms_rows(outs[1], ref_final_gain))
     own = [lax.dynamic_slice_in_dim(o, member * rows, rows, axis=0) for o in outs]
-    every = lax.all_gather(finals, "grp", axis=1, tiled=True)
+    first = (member % 2) == 0
+    chosen = jnp.where(first, finals[0], finals[1])
+    every = lax.all_gather(chosen, "grp", axis=0, tiled=True)
+    pair = [(i, i ^ 1) for i in range(members)]
+    mine = jnp.where(first, pol_head, ref_head)
+    theirs = lax.ppermute(jnp.where(first, ref_head, pol_head), "mdl", pair)
     voc_dev = pol_head.shape[0]
-    positions = jnp.arange(every.shape[1], dtype=jnp.int32)
-    vocab = (group * members + member) * voc_dev + jnp.arange(voc_dev, dtype=jnp.int32)
-    pol_terms = vocab_terms(every[0], pol_head, token_ids, vocab)
-    ref_terms = vocab_terms(every[1], ref_head, token_ids, vocab)
-    peaks = lax.pmax(lax.pmax((pol_terms[0], ref_terms[0]), "mdl"), "grp")
-    sums = lax.psum(
-        lax.psum(
-            (
-                pol_terms[1] * jnp.exp(pol_terms[0] - peaks[0]),
-                pol_terms[2],
-                ref_terms[1] * jnp.exp(ref_terms[0] - peaks[1]),
-                ref_terms[2],
-            ),
-            "mdl",
-        ),
-        "grp",
+    positions = jnp.arange(every.shape[0], dtype=jnp.int32)
+    base = group * members
+    vocab = jnp.concatenate(
+        [
+            (base + member) * voc_dev + jnp.arange(voc_dev, dtype=jnp.int32),
+            (base + (member ^ 1)) * voc_dev + jnp.arange(voc_dev, dtype=jnp.int32),
+        ]
     )
-    pol_logp = sums[1] - peaks[0] - jnp.log(sums[0])
-    ref_logp = sums[3] - peaks[1] - jnp.log(sums[2])
-    rollout_ratio = rollout_totals(pol_logp - ref_logp, positions, lengths)
+    own_terms = jnp.stack(vocab_terms(every, jnp.concatenate([mine, theirs]), token_ids, vocab))
+    other_terms = lax.ppermute(own_terms, "mdl", pair)
+    state = jnp.where(first, jnp.stack([own_terms, other_terms]), jnp.stack([other_terms, own_terms]))
+    rounds = [("mdl", 2), ("mdl", 4), ("mdl", 8), ("mdl", 16), ("mdl", 32), ("grp", 1), ("grp", 2)]
+    for axis, bit in rounds:
+        size = lax.axis_size(axis)
+        other = lax.ppermute(state, axis, [(i, i ^ bit) for i in range(size)])
+        low = (lax.axis_index(axis) & bit) == 0
+        state = merge_terms(jnp.where(low, state, other), jnp.where(low, other, state))
+    logp = state[:, 2] - state[:, 0] - jnp.log(state[:, 1])
+    rollout_ratio = rollout_totals(logp[0] - logp[1], positions, lengths)
     return (own[0], own[1], rollout_ratio)
 
 

time: 922 us -> 480 us (0.52); the launches traced: 908 us -> 479 us
  blocking collectives: 386 us -> 0 us
  waiting for transfers between devices: 435 us -> 379 us
  starting transfers between devices: 0.3 us -> 17.3 us
    psum x2 -> x0, blocking collectives: 261 us -> none  [the longest x1 246 us: per_device(): lax.psum((pol_terms[1] * jnp.exp(pol_terms[0] - peaks[0]), pol_terms[2],...]
    pmax x2 -> x0, blocking collectives: 126 us -> none  [per_device(): peaks = lax.pmax(lax.pmax((pol_terms[0], ref_terms[0]), 'mdl'), 'grp')]
    all_gather x1, waiting for transfers between devices: 153 us -> 75.9 us  [per_device(): every = lax.all_gather(chosen, 'grp', axis=0, tiled=True)]
    ppermute x0 -> x9, waiting for transfers between devices: none -> 20.5 us  [the longest x7 15 us: per_device(): other = lax.ppermute(state, axis, [(i, i ^ bit) for i in range(size)])]
    ppermute x0 -> x9, starting transfers between devices: none -> 17 us  [the longest x7 16.9 us: per_device(): other = lax.ppermute(state, axis, [(i, i ^ bit) for i in range(size)])]
  transfers between devices with their start and end apart: 3 -> 12, of which waited for: 3 -> 12; matrix products, arithmetic and copies ran while one was open for 1% -> 2% of each run, Pallas kernels for 0% -> 0%
where the time goes in v2:
time: 480 us; the launch traced here: 479 us
  waiting for transfers between devices  379 us (79%)
  matrix products  25.3 us (5%)
  other arithmetic  22.3 us (5%)
  local copies, waits for them, and re-layouts  21.4 us (4%)
  starting transfers between devices  17.3 us (4%)
  between operations  14.1 us (3%)
    psum x1, waiting for transfers between devices, per_device(): mixed = lax.psum(partials, 'mdl')  202 us
    all_gather x1, waiting for transfers between devices, per_device(): lax.all_gather(jnp.stack([pol_hidden, ref_hidden]), 'mdl', axis=1, tiled=...  80.4 us
    all_gather x1, waiting for transfers between devices, per_device(): every = lax.all_gather(chosen, 'grp', axis=0, tiled=True)  75.9 us
    ppermute x7, starting transfers between devices, per_device(): other = lax.ppermute(state, axis, [(i, i ^ bit) for i in range(size)])  16.9 us
    ppermute x7, waiting for transfers between devices, per_device(): other = lax.ppermute(state, axis, [(i, i ^ bit) for i in range(size)])  15 us
    slice x1, local copies, waits for them, and re-layouts, per_device(): both_in[i].astype(jnp.float32) + mixed[i]  13.4 us
    dot_general x2, matrix products, mlp_partial(): return jnp.dot(hidden, w_down, preferred_element_type=jnp.float32)  12.6 us
    reduce_sum x3, other arithmetic, rms_rows(): scale = lax.rsqrt(jnp.mean(values * values, axis=-1, keepdims=True) + 1e-05)  10.2 us
  transfers between devices with their start and end apart: 12, of which 12 were waited for; matrix products, arithmetic and copies ran while one was open for 2% of the time, Pallas kernels for 0%

profile of v2, /device:TPU:6, one launch (start us, length us, event | category | flops | bytes accessed | tf_op | source)
XLA Modules:
  0.0 479.3 jit_solution(13688433062827417748)
XLA Ops:
  10.9 80.4 %all-gather.3.cloned.1.call-done = bf16[2,256,4096]{2,0,1:T(2,128)(2,1)} async-done(((bf16[2,4,4096]{2,0,1:T(2,128)(2,1)}), bf16[2,256,4096]{2,0,1:T(2,128)(2,1)}) %all-gather.3.cloned.1.call-update) | async-done | bytes 4194320 | tf_op jit(solution)/shard_map/all_gather | solution.py:66
  91.3 13.4 %fusion.61 = (bf16[1,256,4096]{2,0,1:T(2,128)(2,1)S(1)}, bf16[1,256,4096]{2,0,1:T(2,128)(2,1)S(1)}) fusion(bf16[2,256,4096]{2,0,1:T(2,128)(2,1)} %all-gather.3.cloned.1.call-done), kind=kLoop, calls=%fused_computation.138 | loop fusion | bytes 8388608 | tf_op jit(solution)/shard_map/slice | solution.py:72
  104.7 5.4 %fusion.6 = (f32[256]{0:T(256)S(1)}, bf16[256,4096]{1,0:T(8,128)(2,1)S(1)}, f32[256]{0:T(256)S(1)}, bf16[256,4096]{1,0:T(8,128)(2,1)S(1)}) fusion(bf16[1,256,4096]{2,0,1:T(2,128)(2,1)S(1)} %get-tuple-element.30, bf16[1,256,4096]{2,0,1:T(2,128)(2,1)S(1)} %get-tuple-element.29), kind=kLoop, calls=%fused_computation.16 | loop fusion | flops 6290944 | bytes 8390656 | tf_op jit(solution)/shard_map/reduce_sum | solution.py:9
  111.5 1.6 fusion.29
  113.1 6.6 %fusion.22 = f32[256,4096]{1,0:T(8,128)} fusion(bf16[172,4096]{1,0:T(8,128)(2,1)S(1)} %copy-done, bf16[4096,172]{0,1:T(8,128)(2,1)} %param.23, bf16[256,4096]{1,0:T(8,128)(2,1)} %copy-done.2, f32[4096]{0:T(1024)} %convert_element_type.62, f32[256]{0:T(256)} %copy-done.12, f32[256,172]{0,1:T(8,128)} %fusion.29), kind=kOutput, calls=%fused_computation.40 | convolution fusion | flops 725878784 | bytes 9303040 | tf_op jit(solution)/shard_map/dot_general | solution.py:18
  119.7 3.1 fusion.25
  122.8 6.0 %fusion.21 = f32[256,4096]{1,0:T(8,128)} fusion(bf16[172,4096]{1,0:T(8,128)(2,1)S(1)} %copy-done.7, bf16[4096,172]{0,1:T(8,128)(2,1)} %param.26, bf16[256,4096]{1,0:T(8,128)(2,1)S(1)} %get-tuple-element.55, f32[4096]{0:T(1024)S(1)} %convert_element_type.68, f32[256]{0:T(256)} %add_rsqrt_fusion.2, f32[256,172]{0,1:T(8,128)} %fusion.25), kind=kOutput, calls=%fused_computation.39 | convolution fusion | flops 725878784 | bytes 9303040 | tf_op jit(solution)/shard_map/dot_general | solution.py:18
  129.4 202.2 %all-reduce.3.cloned.1.call-done = (f32[256,4096]{1,0:T(8,128)}, f32[256,4096]{1,0:T(8,128)}) async-done(((f32[256,4096]{1,0:T(8,128)}, f32[256,4096]{1,0:T(8,128)}), (f32[256,4096]{1,0:T(8,128)}, f32[256,4096]{1,0:T(8,128)})) %all-reduce.3.cloned.1.call-update) | async-done | bytes 8388624 | tf_op jit(solution)/shard_map/psum | solution.py:71
  331.6 3.8 fusion
  337.9 2.7 fusion.18
  340.6 1.6 copy-done.6
  342.2 3.8 broadcast_select_fusion.1
  346.1 4.3 collective-permute-done
  350.4 75.9 %all-gather.5.cloned.1.call-done = bf16[1024,4096]{1,0:T(8,128)(2,1)} async-done(((bf16[256,4096]{1,0:T(8,128)(2,1)}), bf16[1024,4096]{1,0:T(8,128)(2,1)}) %all-gather.5.cloned.1.call-update) | async-done | bytes 8388624 | tf_op jit(solution)/shard_map/all_gather | solution.py:77
  426.4 8.0 %fusion.63 = (f32[1024]{0:T(1024)S(1)}, f32[1024,500]{0,1:T(8,128)S(1)}) fusion(bf16[1024,4096]{1,0:T(8,128)(2,1)} %all-gather.5.cloned.1.call-done, bf16[250,4096]{1,0:T(8,128)(2,1)S(1)} %collective-permute-done, bf16[250,4096]{1,0:T(8,128)(2,1)} %get-tuple-element.27), kind=kOutput, calls=%fused_computation.140 | convolution fusion | flops 4203006976 | bytes 14536704 | tf_op jit(solution)/shard_map/td,vd->tv/dot_general | solution.py:22
  437.2 3.0 collective-permute-done.2
  441.8 3.9 collective-permute-done.3
  445.8 1.6 collective-permute-start.4
  447.4 2.3 collective-permute-done.4
  449.8 2.6 collective-permute-start.5
  452.6 1.9 collective-permute-done.5
  454.7 5.8 %collective-permute-start.6 = (f32[2,3,1024]{2,0,1:T(2,128)S(1)}, f32[2,3,1024]{2,0,1:T(2,128)S(1)}, u32[]{:S(2)}, u32[]{:S(2)}) collective-permute-start(f32[2,3,1024]{2,0,1:T(2,128)S(1)} %pad_maximum_fusion.4), channel_id=1, source_target_pairs={{0,32},{1,33},{2,34},{3,35},{4,36},{5,37},{6,38},{7,39},{8,40},{9,... | collective-permute-start | bytes 73736 | tf_op jit(solution)/shard_map/ppermute | solution.py:96
  460.6 1.9 collective-permute-done.6
  466.6 2.8 collective-permute-start.8
  (91 shorter events, 20.6 us)
Async XLA Ops:
  7.2 105.9 %copy-start = (bf16[172,4096]{1,0:T(8,128)(2,1)S(1)}, bf16[172,4096]{1,0:T(8,128)(2,1)}, u32[]{:S(2)}) copy-start(bf16[172,4096]{1,0:T(8,128)(2,1)} %param.24) | copy-start | bytes 4227076
  7.2 84.1 %all-gather.3.cloned.1.call-start = ((), (), s32[]{:S(2)}) async-start(), calls=%async_computation | async-start | bytes 4259840 | tf_op jit(solution)/shard_map/all_gather | solution.py:66
  8.9 322.7 %all-reduce.3.cloned.1.call-start = ((), (), s32[]{:S(2)}) async-start(), calls=%async_computation.2 | async-start | bytes 16777216 | tf_op jit(solution)/shard_map/psum | solution.py:71
  104.7 6.8 %copy-start.8 = (f32[4096]{0:T(1024)S(1)}, f32[4096]{0:T(1024)}, u32[]{:S(2)}) copy-start(f32[4096]{0:T(1024)} %convert_element_type.62) | copy-start | bytes 49156
  104.7 6.8 %copy-start.14 = (bf16[4096,172]{0,1:T(8,128)(2,1)S(1)}, bf16[4096,172]{0,1:T(8,128)(2,1)}, u32[]{:S(2)}) copy-start(bf16[4096,172]{0,1:T(8,128)(2,1)} %param.22) | copy-start | bytes 4227076
  110.1 1.3 copy-start.2
  119.7 3.1 copy-start.7
  128.7 297.6 %all-gather.5.cloned.1.call-start = ((), (), s32[]{:S(2)}) async-start(), calls=%async_computation.1 | async-start | bytes 10485760 | tf_op jit(solution)/shard_map/all_gather | solution.py:77
  331.6 4.1 copy-start.5
  335.4 1.4 copy-start.4
  336.6 1.3 copy-start.3
  340.6 1.6 copy-start.6
  346.1 4.4 collective-permute-start
  426.4 8.0 %copy-start.11 = (s32[1024]{0:T(1024)S(1)}, s32[1024]{0:T(1024)}, u32[]{:S(2)}) copy-start(s32[1024]{0:T(1024)} %param.30) | copy-start | bytes 12292
  426.4 46.4 %copy-start.1 = (bf16[172,4096]{1,0:T(8,128)(2,1)S(1)}, bf16[172,4096]{1,0:T(8,128)(2,1)}, u32[]{:S(2)}) copy-start(bf16[172,4096]{1,0:T(8,128)(2,1)} %param.24) | copy-start | bytes 4227076
  434.4 18.0 %copy-start.13 = (s32[16]{0:T(128)S(1)}, s32[16]{0:T(128)}, u32[]{:S(2)}) copy-start(s32[16]{0:T(128)} %param.31) | copy-start | bytes 196
  434.9 1.3 collective-permute-start.1
  436.3 3.9 collective-permute-start.2
  440.3 5.4 %collective-permute-start.3 = (f32[2,3,1024]{2,0,1:T(2,128)S(1)}, f32[2,3,1024]{2,0,1:T(2,128)S(1)}, u32[]{:S(2)}, u32[]{:S(2)}) collective-permute-start(f32[2,3,1024]{2,0,1:T(2,128)S(1)} %pad_maximum_fusion.1), channel_id=1, source_target_pairs={{0,4},{1,5},{2,6},{3,7},{4,0},{5,1},{6,2},{7,3},{8,12},{9,13},{10,... | collective-permute-start | bytes 73736 | tf_op jit(solution)/shard_map/ppermute | solution.py:96
  445.8 3.9 collective-permute-start.4
  449.8 4.8 %collective-permute-start.5 = (f32[2,3,1024]{2,0,1:T(2,128)S(1)}, f32[2,3,1024]{2,0,1:T(2,128)S(1)}, u32[]{:S(2)}, u32[]{:S(2)}) collective-permute-start(f32[2,3,1024]{2,0,1:T(2,128)S(1)} %pad_maximum_fusion.3), channel_id=1, source_target_pairs={{0,16},{1,17},{2,18},{3,19},{4,20},{5,21},{6,22},{7,23},{8,24},{9,... | collective-permute-start | bytes 73736 | tf_op jit(solution)/shard_map/ppermute | solution.py:96
  454.7 7.8 %collective-permute-start.6 = (f32[2,3,1024]{2,0,1:T(2,128)S(1)}, f32[2,3,1024]{2,0,1:T(2,128)S(1)}, u32[]{:S(2)}, u32[]{:S(2)}) collective-permute-start(f32[2,3,1024]{2,0,1:T(2,128)S(1)} %pad_maximum_fusion.4), channel_id=1, source_target_pairs={{0,32},{1,33},{2,34},{3,35},{4,36},{5,37},{6,38},{7,39},{8,40},{9,... | collective-permute-start | bytes 73736 | tf_op jit(solution)/shard_map/ppermute | solution.py:96
  462.6 3.9 collective-permute-start.7
  466.6 5.4 %collective-permute-start.8 = (f32[2,3,1024]{2,0,1:T(2,128)S(1)}, f32[2,3,1024]{2,0,1:T(2,128)S(1)}, u32[]{:S(2)}, u32[]{:S(2)}) collective-permute-start(f32[2,3,1024]{2,0,1:T(2,128)S(1)} %pad_maximum_fusion.6), channel_id=1, source_target_pairs={{0,128},{64,192},{128,0},{192,64},{1,129},{65,193},{129,1},{193,65... | collective-permute-start | bytes 73736 | tf_op jit(solution)/shard_map/ppermute | solution.py:96
  (3 other events, 2.7 us)
Sparse Core Ops, SparseCore 0:
  10.8 80.4 all-gather.2
  128.9 202.6 all-reduce.2
  340.8 85.5 all-gather.4

commit v3 on v2

v3 whole, which is shorter than its diff:
```python
import jax
import jax.numpy as jnp
from jax import lax
from jax.sharding import Mesh
from jax.sharding import PartitionSpec as P

SWAP = [(0, 1), (1, 0)]


def rms_rows(rows, gain):
    values = rows.astype(jnp.float32)
    scale = lax.rsqrt(jnp.mean(values * values, axis=-1, keepdims=True) + 1e-05)
    return (values * scale * gain.astype(jnp.float32)).astype(jnp.bfloat16)


def mlp_partial(piece, gain, w_gate, w_up, w_down):
    normed = rms_rows(piece, gain)
    gate = jnp.dot(normed, w_gate, preferred_element_type=jnp.float32)
    upper = jnp.dot(normed, w_up, preferred_element_type=jnp.float32)
    hidden = (jax.nn.silu(gate) * upper).astype(jnp.bfloat16)
    return jnp.dot(hidden, w_down, preferred_element_type=jnp.float32)


def vocab_terms(token_rows, head_rows, targets, vocab):
    logits = jnp.einsum("td,vd->tv", token_rows, head_rows, preferred_element_type=jnp.float32)
    peak = jnp.max(logits, axis=1)
    total = jnp.sum(jnp.exp(logits - peak[:, None]), axis=1)
    target = jnp.sum(jnp.where(targets[:, None] == vocab[None, :], logits, 0.0), axis=1)
    return (peak, total, target)


def merge_terms(lo, hi):
    peak = jnp.maximum(lo[:, 0], hi[:, 0])
    total = lo[:, 1] * jnp.exp(lo[:, 0] - peak) + hi[:, 1] * jnp.exp(hi[:, 0] - peak)
    return jnp.stack([peak, total, lo[:, 2] + hi[:, 2]], axis=1)


def rollout_totals(log_ratio, positions, lengths):
    ends = jnp.cumsum(lengths)
    owner = jnp.sum((positions[:, None] >= ends[None, :]).astype(jnp.int32), axis=1)
    onehot = (owner[:, None] == jnp.arange(lengths.shape[0], dtype=jnp.int32)[None, :]).astype(
        jnp.float32
    )
    return jnp.sum(log_ratio[:, None] * onehot, axis=0)


def pick(first, pol, ref):
    return jnp.where(first, pol, ref), jnp.where(first, ref, pol)


def per_device(
    pol_hidden,
    ref_hidden,
    pol_mlp_gain,
    ref_mlp_gain,
    pol_final_gain,
    ref_final_gain,
    pol_gate,
    pol_up,
    pol_down,
    ref_gate,
    ref_up,
    ref_down,
    pol_head,
    ref_head,
    token_ids,
    lengths,
):
    rows = pol_hidden.shape[0]
    core = lax.axis_index("core")
    spot = lax.axis_index("zx")
    group = lax.axis_index("grp")
    first = core == 0
    per_group = lax.axis_size("zx") * 2
    member = spot * 2 + core
    partner = spot * 2 + (1 - core)

    keep_w, give_w = pick(first, jnp.stack([pol_gate, pol_up]), jnp.stack([ref_gate, ref_up]))
    keep_d, give_d = pick(first, pol_down, ref_down)
    got_w = lax.ppermute(give_w, "core", SWAP)
    got_d = lax.ppermute(give_d, "core", SWAP)
    keep_h, give_h = pick(first, pol_hidden, ref_hidden)
    got_h = lax.ppermute(give_h, "core", SWAP)
    pair_rows = jnp.where(
        first, jnp.concatenate([keep_h, got_h]), jnp.concatenate([got_h, keep_h])
    )
    group_rows = lax.all_gather(pair_rows, "zx", axis=0, tiled=True)
    mlp_gain = jnp.where(first, pol_mlp_gain, ref_mlp_gain)
    partial = mlp_partial(group_rows, mlp_gain, keep_w[0], keep_w[1], keep_d) + mlp_partial(
        group_rows, mlp_gain, got_w[0], got_w[1], got_d
    )
    mixed = lax.psum(partial, "zx")
    out = (group_rows.astype(jnp.float32) + mixed).astype(jnp.bfloat16)
    final = rms_rows(out, jnp.where(first, pol_final_gain, ref_final_gain))
    mine_out = lax.dynamic_slice_in_dim(out, member * rows, rows, axis=0)
    sent_out = lax.ppermute(lax.dynamic_slice_in_dim(out, partner * rows, rows, axis=0), "core", SWAP)
    pol_out = jnp.where(first, mine_out, sent_out)
    ref_out = jnp.where(first, sent_out, mine_out)

    every = lax.all_gather(final, "grp", axis=0, tiled=True)
    keep_v, give_v = pick(first, pol_head, ref_head)
    got_v = lax.ppermute(give_v, "core", SWAP)
    voc_dev = pol_head.shape[0]
    positions = jnp.arange(every.shape[0], dtype=jnp.int32)
    base = group * per_group
    vocab = jnp.concatenate(
        [
            (base + member) * voc_dev + jnp.arange(voc_dev, dtype=jnp.int32),
            (base + partner) * voc_dev + jnp.arange(voc_dev, dtype=jnp.int32),
        ]
    )
    own_terms = jnp.stack(vocab_terms(every, jnp.concatenate([keep_v, got_v]), token_ids, vocab))
    other_terms = lax.ppermute(own_terms, "core", SWAP)
    state = jnp.where(first, jnp.stack([own_terms, other_terms]), jnp.stack([other_terms, own_terms]))
    rounds = [("zx", 1), ("zx", 2), ("zx", 4), ("zx", 8), ("zx", 16), ("grp", 1), ("grp", 2)]
    for axis, bit in rounds:
        size = lax.axis_size(axis)
        other = lax.ppermute(state, axis, [(i, i ^ bit) for i in range(size)])
        low = (lax.axis_index(axis) & bit) == 0
        state = merge_terms(jnp.where(low, state, other), jnp.where(low, other, state))
    logp = state[:, 2] - state[:, 0] - jnp.log(state[:, 1])
    rollout_ratio = rollout_totals(logp[0] - logp[1], positions, lengths)
    return (pol_out, ref_out, rollout_ratio)


def solution(mesh):
    groups, members = mesh.devices.shape
    split = Mesh(mesh.devices.reshape(groups, members // 2, 2), ("grp", "zx", "core"))
    rows = P(("grp", "zx", "core"), None)
    units = ("zx", "core")
    placed = (
        rows,
        rows,
        P(),
        P(),
        P(),
        P(),
        P(None, units),
        P(None, units),
        P(units, None),
        P(None, units),
        P(None, units),
        P(units, None),
        rows,
        rows,
        P(),
        P(),
    )
    return jax.shard_map(
        per_device,
        mesh=split,
        in_specs=placed,
        out_specs=(rows, rows, P()),
        check_vma=False,
    )
```

time: 480 us -> 419 us (0.87)
  waiting for transfers between devices: 379 us -> 319 us
  local copies, waits for them, and re-layouts: 21.4 us -> 16.4 us
    psum x1, waiting for transfers between devices: 202 us -> 161 us  [per_device(): mixed = lax.psum(partial, 'zx')]
    all_gather x2, waiting for transfers between devices: 156 us -> 133 us  [the longest x1 74.6 us: per_device(): every = lax.all_gather(final, 'grp', axis=0, tiled=True)]
    select_n x2 -> x6, other arithmetic: 6.53 us -> 12.6 us  [the longest x4 10.4 us: pick(): return (jnp.where(first, pol, ref), jnp.where(first, ref, pol))]
    reduce_sum x3 -> x2, other arithmetic: 10.2 us -> 5.25 us  [rms_rows(): scale = lax.rsqrt(jnp.mean(values * values, axis=-1, keepdims=True) + 1e-05)]
    ppermute x2 -> x6, waiting for transfers between devices: 5.44 us -> 10 us  [the longest x1 4.29 us: per_device(): got_v = lax.ppermute(give_v, 'core', SWAP)]
  transfers between devices with their start and end apart: 12 -> 16, of which waited for: 12 -> 14; matrix products, arithmetic and copies ran while one was open for 2% -> 9% of each run, Pallas kernels for 0% -> 0%
where the time goes in v3:
time: 419 us; the launch traced here: 418 us
  waiting for transfers between devices  319 us (76%)
  matrix products  28.6 us (7%)
  other arithmetic  22 us (5%)
  starting transfers between devices  17.9 us (4%)
  local copies, waits for them, and re-layouts  16.4 us (4%)
  between operations  14.1 us (3%)
    psum x1, waiting for transfers between devices, per_device(): mixed = lax.psum(partial, 'zx')  161 us
    all_gather x1, waiting for transfers between devices, per_device(): every = lax.all_gather(final, 'grp', axis=0, tiled=True)  74.6 us
    all_gather x1, waiting for transfers between devices, per_device(): group_rows = lax.all_gather(pair_rows, 'zx', axis=0, tiled=True)  58.3 us
    ppermute x7, starting transfers between devices, per_device(): other = lax.ppermute(state, axis, [(i, i ^ bit) for i in range(size)])  16.9 us
    ppermute x7, waiting for transfers between devices, per_device(): other = lax.ppermute(state, axis, [(i, i ^ bit) for i in range(size)])  15.5 us
    dot_general x2, matrix products, mlp_partial(): return jnp.dot(hidden, w_down, preferred_element_type=jnp.float32)  14.8 us
    select_n x4, other arithmetic, pick(): return (jnp.where(first, pol, ref), jnp.where(first, ref, pol))  10.4 us
    slice x1, local copies, waits for them, and re-layouts, per_device(): got_w[0]  8.8 us
  transfers between devices with their start and end apart: 16, of which 14 were waited for; matrix products, arithmetic and copies ran while one was open for 9% of the time, Pallas kernels for 0%

profile of v3, /device:TPU:6, one launch (start us, length us, event | category | flops | bytes accessed | tf_op | source)
XLA Modules:
  0.0 418.3 jit_solution(1314656798075704808)
XLA Ops:
  10.1 4.5 %broadcast_select_fusion = (bf16[2,4096,172]{1,2,0:T(8,128)(2,1)S(1)}, bf16[2,4096,172]{1,2,0:T(8,128)(2,1)}) fusion(pred[]{:T(512)S(6)} %eq.50, bf16[1,4096,172]{1,2,0:T(8,128)(2,1)} %bitcast.61, bf16[1,4096,172]{1,2,0:T(8,128)(2,1)} %bitcast.62, bf16[1,4096,172]{1,2,0:T(8,128)(2,1)} %bitcast.63, bf16[1,4096,172]{1,2,0:T(8,128)(2,1)} %bitcast.64), kind=kLoop, calls=%fused_computation.19 | loop fusion | flops 5636096 | bytes 11272193 | tf_op jit(solution)/shard_map/jit(_where)/select_n | solution.py:48
  14.6 2.9 copy.46
  19.5 3.4 collective-permute-done.1
  22.8 8.8 %fusion.50 = (bf16[1,4096,172]{1,0,2:T(2,128)(2,1)}, bf16[1,4096,172]{1,0,2:T(2,128)(2,1)}) fusion(bf16[2,4096,172]{1,0,2:T(2,128)(2,1)S(1)} %collective-permute-done.1), kind=kLoop, calls=%fused_computation.133 | loop fusion | bytes 5636096 | tf_op jit(solution)/shard_map/slice | solution.py:90
  31.6 58.3 %all-gather.3.cloned.1.call-done = bf16[256,4096]{1,0:T(8,128)(2,1)} async-done(((bf16[8,4096]{1,0:T(8,128)(2,1)}), bf16[256,4096]{1,0:T(8,128)(2,1)}) %all-gather.3.cloned.1.call-update) | async-done | bytes 2097168 | tf_op jit(solution)/shard_map/all_gather | solution.py:87
  90.0 2.2 fusion.3
  92.3 3.1 fusion.12
  95.4 2.7 fusion.13
  98.1 6.0 %fusion.15 = f32[256,4096]{1,0:T(8,128)} fusion(bf16[172,4096]{1,0:T(8,128)(2,1)S(1)} %copy-done.2, bf16[172,4096]{1,0:T(8,128)(2,1)} %param.27, pred[]{:T(512)S(6)} %eq.50, bf16[2,4096,172]{1,2,0:T(8,128)(2,1)} %get-tuple-element.20, f32[256,172]{0,1:T(8,128)} %fusion.12, bf16[256,4096]{1,0:T(8,128)(2,1)S(1)} %copy-done, ...), kind=kOutput, calls=%fused_computation.33 | convolution fusion | flops 726583296 | bytes 10781697 | tf_op jit(solution)/shard_map/dot_general | solution.py:21
  104.0 8.9 %convolution_add_fusion = f32[256,4096]{1,0:T(8,128)} fusion(f32[256,4096]{1,0:T(8,128)} %fusion.15, bf16[172,4096]{1,0:T(8,128)(2,1)} %collective-permute-done.2, f32[256,172]{0,1:T(8,128)} %fusion.13, bf16[1,4096,172]{1,0,2:T(2,128)(2,1)} %get-tuple-element.23, bf16[256,4096]{1,0:T(8,128)(2,1)S(1)} %copy-done, f32[4096]{0:T(1024)S(1)} %select_convert_fusion.1, ...), kind=kOutput, calls=%fused_computation.3 | convolution fusion | flops 726927360 | bytes 13497344 | tf_op jit(solution)/shard_map/dot_general | solution.py:21
  113.6 161.0 %all-reduce.2.cloned.1.call-done = f32[256,4096]{1,0:T(8,128)} async-done(((f32[256,4096]{1,0:T(8,128)}), f32[256,4096]{1,0:T(8,128)}) %all-reduce.2.cloned.1.call-update) | async-done | bytes 4194320 | tf_op jit(solution)/shard_map/psum | solution.py:92
  274.6 3.0 fusion
  279.0 2.1 fusion.2
  282.7 3.8 broadcast_select_fusion.3
  286.6 4.3 %collective-permute-done.4 = bf16[250,4096]{1,0:T(8,128)(2,1)S(1)} collective-permute-done((bf16[250,4096]{1,0:T(8,128)(2,1)}, bf16[250,4096]{1,0:T(8,128)(2,1)S(1)}, u32[]{:S(2)}, u32[]{:S(2)}) %collective-permute-start.4) | collective-permute-done | bytes 2048032 | tf_op jit(solution)/shard_map/ppermute | solution.py:102
  290.9 74.6 %all-gather.5.cloned.1.call-done = bf16[1024,4096]{1,0:T(8,128)(2,1)} async-done(((bf16[256,4096]{1,0:T(8,128)(2,1)}), bf16[1024,4096]{1,0:T(8,128)(2,1)}) %all-gather.5.cloned.1.call-update) | async-done | bytes 8388624 | tf_op jit(solution)/shard_map/all_gather | solution.py:100
  365.5 7.9 %fusion.52 = (f32[1024]{0:T(1024)S(1)}, f32[1024,500]{0,1:T(8,128)S(1)}) fusion(bf16[1024,4096]{1,0:T(8,128)(2,1)} %all-gather.5.cloned.1.call-done, bf16[250,4096]{1,0:T(8,128)(2,1)S(1)} %collective-permute-done.4, bf16[250,4096]{1,0:T(8,128)(2,1)} %get-tuple-element.21), kind=kOutput, calls=%fused_computation.135 | convolution fusion | flops 4203006976 | bytes 14536704 | tf_op jit(solution)/shard_map/td,vd->tv/dot_general | solution.py:25
  376.2 3.0 collective-permute-done.6
  380.9 3.9 collective-permute-done.7
  386.5 2.3 collective-permute-done.8
  388.8 2.6 collective-permute-start.9
  391.7 1.9 collective-permute-done.9
  393.7 5.8 %collective-permute-start.10 = (f32[2,3,1024]{2,0,1:T(2,128)S(1)}, f32[2,3,1024]{2,0,1:T(2,128)S(1)}, u32[]{:S(2)}, u32[]{:S(2)}) collective-permute-start(f32[2,3,1024]{2,0,1:T(2,128)S(1)} %pad_maximum_fusion.5), channel_id=1, source_target_pairs={{0,32},{2,34},{4,36},{6,38},{8,40},{10,42},{12,44},{14,46},{16,48}... | collective-permute-start | bytes 73736 | tf_op jit(solution)/shard_map/ppermute | solution.py:118
  405.6 2.8 collective-permute-start.12
  (93 shorter events, 24.4 us)
Async XLA Ops:
  7.2 82.8 %all-gather.3.cloned.1.call-start = ((), (), s32[]{:S(2)}) async-start(), calls=%async_computation | async-start | bytes 2162688 | tf_op jit(solution)/shard_map/all_gather | solution.py:87
  8.0 1.3 collective-permute-start
  10.0 264.6 %all-reduce.2.cloned.1.call-start = ((), (), s32[]{:S(2)}) async-start(), calls=%async_computation.1 | async-start | bytes 8388608 | tf_op jit(solution)/shard_map/psum | solution.py:92
  14.6 3.2 copy-start.2
  14.6 3.2 copy-start.3
  17.5 1.9 copy-start.7
  17.6 5.3 %collective-permute-start.1 = (bf16[2,4096,172]{1,0,2:T(2,128)(2,1)S(1)}, bf16[2,4096,172]{1,0,2:T(2,128)(2,1)S(1)}, u32[]{:S(2)}, u32[]{:S(2)}) collective-permute-start(bf16[2,4096,172]{1,0,2:T(2,128)(2,1)S(1)} %copy.46), channel_id=1, source_target_pairs={{0,1},{1,0},{2,3},{3,2},{4,5},{5,4},{6,7},{7,6},{8,9},{9,8},{10,11... | collective-permute-start | bytes 8454152 | tf_op jit(solution)/shard_map/ppermute | solution.py:80
  19.1 84.9 %collective-permute-start.2 = (bf16[172,4096]{1,0:T(8,128)(2,1)}, bf16[172,4096]{1,0:T(8,128)(2,1)}, u32[]{:S(2)}, u32[]{:S(2)}) collective-permute-start(bf16[172,4096]{1,0:T(8,128)(2,1)} %broadcast_select_fusion.4), channel_id=1, source_target_pairs={{0,1},{1,0},{2,3},{3,2},{4,5},{5,4},{6,7},{7,6},{8,9},{9,8},{10,11... | collective-permute-start | bytes 4227080 | tf_op jit(solution)/shard_map/ppermute | solution.py:81
  90.0 2.3 copy-start
  92.2 3.2 copy-start.6
  92.2 3.1 copy-start.4
  112.9 252.5 %all-gather.5.cloned.1.call-start = ((), (), s32[]{:S(2)}) async-start(), calls=%async_computation.2 | async-start | bytes 10485760 | tf_op jit(solution)/shard_map/all_gather | solution.py:100
  286.5 4.4 %collective-permute-start.4 = (bf16[250,4096]{1,0:T(8,128)(2,1)}, bf16[250,4096]{1,0:T(8,128)(2,1)S(1)}, u32[]{:S(2)}, u32[]{:S(2)}) collective-permute-start(bf16[250,4096]{1,0:T(8,128)(2,1)} %get-tuple-element.22), channel_id=1, source_target_pairs={{0,1},{1,0},{2,3},{3,2},{4,5},{5,4},{6,7},{7,6},{8,9},{9,8},{10,11... | collective-permute-start | bytes 6144008 | tf_op jit(solution)/shard_map/ppermute | solution.py:102
  365.5 7.9 %copy-start.11 = (s32[1024]{0:T(1024)S(1)}, s32[1024]{0:T(1024)}, u32[]{:S(2)}) copy-start(s32[1024]{0:T(1024)} %param.30) | copy-start | bytes 12292
  373.4 18.0 %copy-start.12 = (s32[16]{0:T(128)S(1)}, s32[16]{0:T(128)}, u32[]{:S(2)}) copy-start(s32[16]{0:T(128)} %param.31) | copy-start | bytes 196
  374.0 1.3 collective-permute-start.5
  375.3 3.9 collective-permute-start.6
  379.3 5.4 %collective-permute-start.7 = (f32[2,3,1024]{2,0,1:T(2,128)S(1)}, f32[2,3,1024]{2,0,1:T(2,128)S(1)}, u32[]{:S(2)}, u32[]{:S(2)}) collective-permute-start(f32[2,3,1024]{2,0,1:T(2,128)S(1)} %pad_maximum_fusion.2), channel_id=1, source_target_pairs={{0,4},{2,6},{4,0},{6,2},{8,12},{10,14},{12,8},{14,10},{16,20},{18,... | collective-permute-start | bytes 73736 | tf_op jit(solution)/shard_map/ppermute | solution.py:118
  384.8 3.9 collective-permute-start.8
  388.8 4.8 %collective-permute-start.9 = (f32[2,3,1024]{2,0,1:T(2,128)S(1)}, f32[2,3,1024]{2,0,1:T(2,128)S(1)}, u32[]{:S(2)}, u32[]{:S(2)}) collective-permute-start(f32[2,3,1024]{2,0,1:T(2,128)S(1)} %pad_maximum_fusion.4), channel_id=1, source_target_pairs={{0,16},{2,18},{4,20},{6,22},{8,24},{10,26},{12,28},{14,30},{16,0},... | collective-permute-start | bytes 73736 | tf_op jit(solution)/shard_map/ppermute | solution.py:118
  393.7 7.8 %collective-permute-start.10 = (f32[2,3,1024]{2,0,1:T(2,128)S(1)}, f32[2,3,1024]{2,0,1:T(2,128)S(1)}, u32[]{:S(2)}, u32[]{:S(2)}) collective-permute-start(f32[2,3,1024]{2,0,1:T(2,128)S(1)} %pad_maximum_fusion.5), channel_id=1, source_target_pairs={{0,32},{2,34},{4,36},{6,38},{8,40},{10,42},{12,44},{14,46},{16,48}... | collective-permute-start | bytes 73736 | tf_op jit(solution)/shard_map/ppermute | solution.py:118
  401.6 3.9 collective-permute-start.11
  404.0 4.4 %collective-permute-start.3 = (bf16[4,4096]{1,0:T(4,128)(2,1)S(1)}, bf16[4,4096]{1,0:T(4,128)(2,1)S(1)}, u32[]{:S(2)}, u32[]{:S(2)}) collective-permute-start(bf16[4,4096]{1,0:T(4,128)(2,1)S(1)} %constant_dynamic-slice_fusion), channel_id=1, source_target_pairs={{0,1},{1,0},{2,3},{3,2},{4,5},{5,4},{6,7},{7,6},{8,9},{9,8},{10,11... | collective-permute-start | bytes 98312 | tf_op jit(solution)/shard_map/ppermute | solution.py:96
  405.6 5.4 %collective-permute-start.12 = (f32[2,3,1024]{2,0,1:T(2,128)S(1)}, f32[2,3,1024]{2,0,1:T(2,128)S(1)}, u32[]{:S(2)}, u32[]{:S(2)}) collective-permute-start(f32[2,3,1024]{2,0,1:T(2,128)S(1)} %pad_maximum_fusion.7), channel_id=1, source_target_pairs={{0,128},{64,192},{128,0},{192,64},{1,129},{65,193},{129,1},{193,65... | collective-permute-start | bytes 73736 | tf_op jit(solution)/shard_map/ppermute | solution.py:118
  (5 other events, 6.3 us)
Sparse Core Ops, SparseCore 0:
  10.6 79.3 all-gather.2
  113.1 161.4 all-reduce.1
  281.2 84.2 all-gather.4

commit v4 on v3

--- a/solution.py
+++ b/solution.py
@@ -44,6 +44,43 @@
     return jnp.sum(log_ratio[:, None] * onehot, axis=0)
 
 
+def zx_bits():
+    size = lax.axis_size("zx")
+    return [1 << k for k in reversed(range(size.bit_length() - 1))]
+
+
+def gather_doubling(block):
+    bits = zx_bits()
+    spot = lax.axis_index("zx")
+    held = block.reshape((1,) * len(bits) + block.shape)
+    for bit in [16, 8, 2, 4, 1]:
+        if bit not in bits:
+            continue
+        dim = bits.index(bit)
+        other = lax.ppermute(held, "zx", [(i, i ^ bit) for i in range(lax.axis_size("zx"))])
+        low = (spot & bit) == 0
+        held = jnp.concatenate([jnp.where(low, held, other), jnp.where(low, other, held)], axis=dim)
+    return held.reshape((-1,) + block.shape[1:])
+
+
+def scatter_halving(full):
+    bits = zx_bits()
+    spot = lax.axis_index("zx")
+    held = full.reshape((2,) * len(bits) + (-1,) + full.shape[1:])
+    for bit in [1, 4, 2, 8, 16]:
+        if bit not in bits:
+            continue
+        dim = bits.index(bit)
+        lower = lax.slice_in_dim(held, 0, 1, axis=dim)
+        upper = lax.slice_in_dim(held, 1, 2, axis=dim)
+        low = (spot & bit) == 0
+        other = lax.ppermute(
+            jnp.where(low, upper, lower), "zx", [(i, i ^ bit) for i in range(lax.axis_size("zx"))]
+        )
+        held = jnp.where(low, lower, upper) + other
+    return held.reshape((-1,) + full.shape[1:])
+
+
 def pick(first, pol, ref):
     return jnp.where(first, pol, ref), jnp.where(first, ref, pol)
 
@@ -84,16 +121,16 @@
     pair_rows = jnp.where(
         first, jnp.concatenate([keep_h, got_h]), jnp.concatenate([got_h, keep_h])
     )
-    group_rows = lax.all_gather(pair_rows, "zx", axis=0, tiled=True)
+    group_rows = gather_doubling(pair_rows)
     mlp_gain = jnp.where(first, pol_mlp_gain, ref_mlp_gain)
     partial = mlp_partial(group_rows, mlp_gain, keep_w[0], keep_w[1], keep_d) + mlp_partial(
         group_rows, mlp_gain, got_w[0], got_w[1], got_d
     )
-    mixed = lax.psum(partial, "zx")
-    out = (group_rows.astype(jnp.float32) + mixed).astype(jnp.bfloat16)
-    final = rms_rows(out, jnp.where(first, pol_final_gain, ref_final_gain))
-    mine_out = lax.dynamic_slice_in_dim(out, member * rows, rows, axis=0)
-    sent_out = lax.ppermute(lax.dynamic_slice_in_dim(out, partner * rows, rows, axis=0), "core", SWAP)
+    mixed = scatter_halving(partial)
+    out = (pair_rows.astype(jnp.float32) + mixed).astype(jnp.bfloat16)
+    final = gather_doubling(rms_rows(out, jnp.where(first, pol_final_gain, ref_final_gain)))
+    mine_out = lax.dynamic_slice_in_dim(out, core * rows, rows, axis=0)
+    sent_out = lax.ppermute(lax.dynamic_slice_in_dim(out, (1 - core) * rows, rows, axis=0), "core", SWAP)
     pol_out = jnp.where(first, mine_out, sent_out)
     ref_out = jnp.where(first, sent_out, mine_out)
 

time: 419 us -> 409 us (0.976); the launches traced: 418 us -> 402 us
  waiting for transfers between devices: 319 us -> 270 us
  starting transfers between devices: 17.9 us -> 50.8 us
    ppermute x1 -> x16, waiting for transfers between devices: 0.01 us -> 172 us  [the longest x5 87.9 us: scatter_halving(): lax.ppermute(jnp.where(low, upper, lower), 'zx', [(i, i ^ bit) for i in r...]
    psum x1 -> x0, waiting for transfers between devices: 161 us -> none  [per_device(): mixed = lax.psum(partial, 'zx')]
    all_gather x1 -> x0, waiting for transfers between devices: 58.3 us -> none  [per_device(): group_rows = lax.all_gather(pair_rows, 'zx', axis=0, tiled=True)]
    ppermute x1 -> x16, starting transfers between devices: 0.09 us -> 33.2 us  [the longest x10 20.9 us: gather_doubling(): lax.ppermute(held, 'zx', [(i, i ^ bit) for i in range(lax.axis_size('zx'))])]
    reduce_sum x2, other arithmetic: 5.25 us -> 0.7 us  [rms_rows(): scale = lax.rsqrt(jnp.mean(values * values, axis=-1, keepdims=True) + 1e-05)]
    select_n x0 -> x15, other arithmetic: none -> 4.42 us  [the longest x5 2.81 us: scatter_halving(): jnp.where(low, upper, lower)]
  transfers between devices with their start and end apart: 16 -> 29, of which waited for: 14 -> 26; matrix products, arithmetic and copies ran while one was open for 9% -> 9% of each run, Pallas kernels for 0% -> 0%
where the time goes in v4:
time: 409 us; the launch traced here: 402 us
  waiting for transfers between devices  270 us (66%)
  starting transfers between devices  50.8 us (12%)
  matrix products  26.4 us (6%)
  other arithmetic  22.3 us (5%)
  local copies, waits for them, and re-layouts  17.4 us (4%)
  between operations  15.1 us (4%)
    ppermute x5, waiting for transfers between devices, scatter_halving(): lax.ppermute(jnp.where(low, upper, lower), 'zx', [(i, i ^ bit) for i in r...  87.9 us
    ppermute x10, waiting for transfers between devices, gather_doubling(): lax.ppermute(held, 'zx', [(i, i ^ bit) for i in range(lax.axis_size('zx'))])  83.8 us
    all_gather x1, waiting for transfers between devices, per_device(): every = lax.all_gather(final, 'grp', axis=0, tiled=True)  74.2 us
    ppermute x10, starting transfers between devices, gather_doubling(): lax.ppermute(held, 'zx', [(i, i ^ bit) for i in range(lax.axis_size('zx'))])  20.9 us
    ppermute x7, waiting for transfers between devices, per_device(): other = lax.ppermute(state, axis, [(i, i ^ bit) for i in range(size)])  17.1 us
    ppermute x7, starting transfers between devices, per_device(): other = lax.ppermute(state, axis, [(i, i ^ bit) for i in range(size)])  16.9 us
    dot_general x2, matrix products, mlp_partial(): return jnp.dot(hidden, w_down, preferred_element_type=jnp.float32)  14.7 us
    ppermute x5, starting transfers between devices, scatter_halving(): lax.ppermute(jnp.where(low, upper, lower), 'zx', [(i, i ^ bit) for i in r...  12.2 us
  transfers between devices with their start and end apart: 29, of which 26 were waited for; matrix products, arithmetic and copies ran while one was open for 9% of the time, Pallas kernels for 0%

profile of v4, /device:TPU:6, one launch (start us, length us, event | category | flops | bytes accessed | tf_op | source)
XLA Modules:
  0.0 401.9 jit_solution(477910055364697675)
XLA Ops:
  9.5 7.3 %collective-permute-start.1 = (bf16[1,1,1,1,1,8,4096]{6,5,4,3,2,1,0:T(8,128)(2,1)S(1)}, bf16[1,1,1,1,1,8,4096]{6,5,4,3,2,1,0:T(8,128)(2,1)S(1)}, u32[]{:S(2)}, u32[]{:S(2)}) collective-permute-start(bf16[1,1,1,1,1,8,4096]{6,5,4,3,2,1,0:T(8,128)(2,1)S(1)} %maximum_select_fusion.1), channel_id=1, source_target_pairs={{0,32},{2,34},{4,36},{6,38},{8,40},{10,42},{12,44},{14,46},{16,48}... | collective-permute-start | bytes 196616 | tf_op jit(solution)/shard_map/ppermute | solution.py:60
  22.6 5.5 %collective-permute-done.2 = bf16[2,1,1,1,1,8,4096]{6,5,4,3,2,1,0:T(8,128)(2,1)S(1)} collective-permute-done((bf16[2,1,1,1,1,8,4096]{6,5,4,3,2,1,0:T(8,128)(2,1)S(1)}, bf16[2,1,1,1,1,8,4096]{6,5,4,3,2,1,0:T(8,128)(2,1)S(1)}, u32[]{:S(2)}, u32[]{:S(2)}) %collective-permute-start.2) | collective-permute-done | bytes 131104 | tf_op jit(solution)/shard_map/ppermute | solution.py:60
  29.7 7.8 %collective-permute-done.3 = bf16[2,2,1,1,1,8,4096]{6,5,4,3,2,1,0:T(8,128)(2,1)S(1)} collective-permute-done((bf16[2,2,1,1,1,8,4096]{6,5,4,3,2,1,0:T(8,128)(2,1)S(1)}, bf16[2,2,1,1,1,8,4096]{6,5,4,3,2,1,0:T(8,128)(2,1)S(1)}, u32[]{:S(2)}, u32[]{:S(2)}) %collective-permute-start.3) | collective-permute-done | bytes 262176 | tf_op jit(solution)/shard_map/ppermute | solution.py:60
  41.6 4.6 %copy.46 = bf16[2,4096,172]{1,0,2:T(2,128)(2,1)} copy(bf16[2,4096,172]{1,2,0:T(8,128)(2,1)S(1)} %get-tuple-element.20) | data formatting | bytes 5636096 | tf_op jit(solution)/shard_map/jit(_where)/select_n | solution.py:85
  54.7 20.6 %collective-permute-done.5 = bf16[2,2,2,2,1,8,4096]{6,5,4,3,2,1,0:T(8,128)(2,1)S(1)} collective-permute-done((bf16[2,2,2,2,1,8,4096]{6,5,4,3,2,1,0:T(8,128)(2,1)}, bf16[2,2,2,2,1,8,4096]{6,5,4,3,2,1,0:T(8,128)(2,1)S(1)}, u32[]{:S(2)}, u32[]{:S(2)}) %collective-permute-start.5) | collective-permute-done | bytes 1048608 | tf_op jit(solution)/shard_map/ppermute | solution.py:60
  79.4 5.9 %fusion.11 = f32[256,4096]{1,0:T(8,128)} fusion(bf16[172,4096]{1,0:T(8,128)(2,1)S(1)} %copy-done.2, bf16[172,4096]{1,0:T(8,128)(2,1)} %param.27, pred[]{:T(512)S(6)} %eq.28, f32[256,172]{0,1:T(8,128)} %fusion.7, bf16[256,4096]{1,0:T(8,128)(2,1)S(1)} %bitcast.76, bf16[2,4096,172]{1,2,0:T(8,128)(2,1)} %get-tuple-element.21), kind=kOutput, calls=%fused_computation.30 | convolution fusion | flops 722388992 | bytes 10764289 | tf_op jit(solution)/shard_map/dot_general | solution.py:21
  85.3 10.0 %fusion.34 = (bf16[1,4096,172]{1,0,2:T(2,128)(2,1)}, bf16[1,4096,172]{1,0,2:T(2,128)(2,1)S(1)}) fusion(bf16[2,4096,172]{1,0,2:T(2,128)(2,1)} %collective-permute-done.6), kind=kLoop, calls=%fused_computation.166 | loop fusion | bytes 5636096 | tf_op jit(solution)/shard_map/slice | solution.py:127
  97.2 8.8 %convolution_add_fusion = f32[256,4096]{1,0:T(8,128)} fusion(f32[256,4096]{1,0:T(8,128)} %fusion.11, bf16[172,4096]{1,0:T(8,128)(2,1)} %collective-permute-done.7, f32[256,172]{0,1:T(8,128)S(1)} %fusion.9, bf16[256,4096]{1,0:T(8,128)(2,1)S(1)} %bitcast.78, bf16[1,4096,172]{1,0,2:T(2,128)(2,1)} %get-tuple-element.24), kind=kOutput, calls=%fused_computation | convolution fusion | flops 722733056 | bytes 13479936 | tf_op jit(solution)/shard_map/dot_general | solution.py:21
  109.5 43.9 %collective-permute-done.8 = f32[2,2,2,2,1,8,4096]{6,5,4,3,2,1,0:T(8,128)S(1)} collective-permute-done((f32[2,2,2,2,1,8,4096]{6,5,4,3,2,1,0:T(8,128)S(1)}, f32[2,2,2,2,1,8,4096]{6,5,4,3,2,1,0:T(8,128)S(1)}, u32[]{:S(2)}, u32[]{:S(2)}) %collective-permute-start.8) | collective-permute-done | bytes 2097184 | tf_op jit(solution)/shard_map/ppermute | solution.py:77
  155.8 20.4 %collective-permute-done.9 = f32[2,2,1,2,1,8,4096]{6,5,4,3,2,1,0:T(8,128)S(1)} collective-permute-done((f32[2,2,1,2,1,8,4096]{6,5,4,3,2,1,0:T(8,128)S(1)}, f32[2,2,1,2,1,8,4096]{6,5,4,3,2,1,0:T(8,128)S(1)}, u32[]{:S(2)}, u32[]{:S(2)}) %collective-permute-start.9) | collective-permute-done | bytes 1048608 | tf_op jit(solution)/shard_map/ppermute | solution.py:77
  178.1 10.2 %collective-permute-done.10 = f32[2,2,1,1,1,8,4096]{6,5,4,3,2,1,0:T(8,128)S(1)} collective-permute-done((f32[2,2,1,1,1,8,4096]{6,5,4,3,2,1,0:T(8,128)S(1)}, f32[2,2,1,1,1,8,4096]{6,5,4,3,2,1,0:T(8,128)S(1)}, u32[]{:S(2)}, u32[]{:S(2)}) %collective-permute-start.10) | collective-permute-done | bytes 524320 | tf_op jit(solution)/shard_map/ppermute | solution.py:77
  192.2 8.3 %collective-permute-done.11 = f32[2,1,1,1,1,8,4096]{6,5,4,3,2,1,0:T(8,128)S(1)} collective-permute-done((f32[2,1,1,1,1,8,4096]{6,5,4,3,2,1,0:T(8,128)S(1)}, f32[2,1,1,1,1,8,4096]{6,5,4,3,2,1,0:T(8,128)S(1)}, u32[]{:S(2)}, u32[]{:S(2)}) %collective-permute-start.11) | collective-permute-done | bytes 262176 | tf_op jit(solution)/shard_map/ppermute | solution.py:77
  200.6 4.1 %collective-permute-start.12 = (f32[1,1,1,1,1,8,4096]{6,5,4,3,2,1,0:T(8,128)S(1)}, f32[1,1,1,1,1,8,4096]{6,5,4,3,2,1,0:T(8,128)S(1)}, u32[]{:S(2)}, u32[]{:S(2)}) collective-permute-start(f32[1,1,1,1,1,8,4096]{6,5,4,3,2,1,0:T(8,128)S(1)} %slice_select_fusion.4), channel_id=1, source_target_pairs={{0,32},{2,34},{4,36},{6,38},{8,40},{10,42},{12,44},{14,46},{16,48}... | collective-permute-start | bytes 393224 | tf_op jit(solution)/shard_map/ppermute | solution.py:77
  204.7 5.1 %collective-permute-done.12 = f32[1,1,1,1,1,8,4096]{6,5,4,3,2,1,0:T(8,128)S(1)} collective-permute-done((f32[1,1,1,1,1,8,4096]{6,5,4,3,2,1,0:T(8,128)S(1)}, f32[1,1,1,1,1,8,4096]{6,5,4,3,2,1,0:T(8,128)S(1)}, u32[]{:S(2)}, u32[]{:S(2)}) %collective-permute-start.12) | collective-permute-done | bytes 131104 | tf_op jit(solution)/shard_map/ppermute | solution.py:77
  210.1 4.1 %collective-permute-start.14 = (bf16[1,1,1,1,1,8,4096]{6,5,4,3,2,1,0:T(8,128)(2,1)S(1)}, bf16[1,1,1,1,1,8,4096]{6,5,4,3,2,1,0:T(8,128)(2,1)S(1)}, u32[]{:S(2)}, u32[]{:S(2)}) collective-permute-start(bf16[1,1,1,1,1,8,4096]{6,5,4,3,2,1,0:T(8,128)(2,1)S(1)} %multiply_convert_fusion.2), channel_id=1, source_target_pairs={{0,32},{2,34},{4,36},{6,38},{8,40},{10,42},{12,44},{14,46},{16,48}... | collective-permute-start | bytes 196616 | tf_op jit(solution)/shard_map/ppermute | solution.py:60
  214.2 4.2 %collective-permute-done.14 = bf16[1,1,1,1,1,8,4096]{6,5,4,3,2,1,0:T(8,128)(2,1)S(1)} collective-permute-done((bf16[1,1,1,1,1,8,4096]{6,5,4,3,2,1,0:T(8,128)(2,1)S(1)}, bf16[1,1,1,1,1,8,4096]{6,5,4,3,2,1,0:T(8,128)(2,1)S(1)}, u32[]{:S(2)}, u32[]{:S(2)}) %collective-permute-start.14) | collective-permute-done | bytes 65568 | tf_op jit(solution)/shard_map/ppermute | solution.py:60
  219.3 6.5 %collective-permute-done.15 = bf16[2,1,1,1,1,8,4096]{6,5,4,3,2,1,0:T(8,128)(2,1)S(1)} collective-permute-done((bf16[2,1,1,1,1,8,4096]{6,5,4,3,2,1,0:T(8,128)(2,1)S(1)}, bf16[2,1,1,1,1,8,4096]{6,5,4,3,2,1,0:T(8,128)(2,1)S(1)}, u32[]{:S(2)}, u32[]{:S(2)}) %collective-permute-start.15) | collective-permute-done | bytes 131104 | tf_op jit(solution)/shard_map/ppermute | solution.py:60
  227.7 6.1 %collective-permute-done.16 = bf16[2,2,1,1,1,8,4096]{6,5,4,3,2,1,0:T(8,128)(2,1)S(1)} collective-permute-done((bf16[2,2,1,1,1,8,4096]{6,5,4,3,2,1,0:T(8,128)(2,1)S(1)}, bf16[2,2,1,1,1,8,4096]{6,5,4,3,2,1,0:T(8,128)(2,1)S(1)}, u32[]{:S(2)}, u32[]{:S(2)}) %collective-permute-start.16) | collective-permute-done | bytes 262176 | tf_op jit(solution)/shard_map/ppermute | solution.py:60
  234.1 9.1 %collective-permute-done.17 = bf16[2,2,1,2,1,8,4096]{6,5,4,3,2,1,0:T(8,128)(2,1)S(1)} collective-permute-done((bf16[2,2,1,2,1,8,4096]{6,5,4,3,2,1,0:T(8,128)(2,1)S(1)}, bf16[2,2,1,2,1,8,4096]{6,5,4,3,2,1,0:T(8,128)(2,1)S(1)}, u32[]{:S(2)}, u32[]{:S(2)}) %collective-permute-start.17) | collective-permute-done | bytes 524320 | tf_op jit(solution)/shard_map/ppermute | solution.py:60
  244.4 17.5 %collective-permute-done.18 = bf16[2,2,2,2,1,8,4096]{6,5,4,3,2,1,0:T(8,128)(2,1)S(1)} collective-permute-done((bf16[2,2,2,2,1,8,4096]{6,5,4,3,2,1,0:T(8,128)(2,1)S(1)}, bf16[2,2,2,2,1,8,4096]{6,5,4,3,2,1,0:T(8,128)(2,1)S(1)}, u32[]{:S(2)}, u32[]{:S(2)}) %collective-permute-start.18) | collective-permute-done | bytes 1048608 | tf_op jit(solution)/shard_map/ppermute | solution.py:60
  269.3 4.4 %collective-permute-done.19 = bf16[250,4096]{1,0:T(8,128)(2,1)} collective-permute-done((bf16[250,4096]{1,0:T(8,128)(2,1)}, bf16[250,4096]{1,0:T(8,128)(2,1)}, u32[]{:S(2)}, u32[]{:S(2)}) %collective-permute-start.19) | collective-permute-done | bytes 2048032 | tf_op jit(solution)/shard_map/ppermute | solution.py:139
  273.7 74.2 %all-gather.2.cloned.1.call-done = bf16[1024,4096]{1,0:T(8,128)(2,1)} async-done(((bf16[256,4096]{1,0:T(8,128)(2,1)}), bf16[1024,4096]{1,0:T(8,128)(2,1)}) %all-gather.2.cloned.1.call-update) | async-done | bytes 8388624 | tf_op jit(solution)/shard_map/all_gather | solution.py:137
  348.0 8.2 %fusion.36 = (f32[1024]{0:T(1024)S(1)}, f32[1024,500]{0,1:T(8,128)S(1)}) fusion(bf16[1024,4096]{1,0:T(8,128)(2,1)} %all-gather.2.cloned.1.call-done, bf16[250,4096]{1,0:T(8,128)(2,1)} %collective-permute-done.19, bf16[250,4096]{1,0:T(8,128)(2,1)} %get-tuple-element.22), kind=kOutput, calls=%fused_computation.168 | convolution fusion | flops 4203006976 | bytes 14536704 | tf_op jit(solution)/shard_map/td,vd->tv/dot_general | solution.py:25
  376.5 5.8 %collective-permute-start.25 = (f32[2,3,1024]{2,0,1:T(2,128)S(1)}, f32[2,3,1024]{2,0,1:T(2,128)S(1)}, u32[]{:S(2)}, u32[]{:S(2)}) collective-permute-start(f32[2,3,1024]{2,0,1:T(2,128)S(1)} %pad_maximum_fusion.15), channel_id=1, source_target_pairs={{0,32},{2,34},{4,36},{6,38},{8,40},{10,42},{12,44},{14,46},{16,48}... | collective-permute-start | bytes 73736 | tf_op jit(solution)/shard_map/ppermute | solution.py:155
  (158 shorter events, 84.0 us)
Async XLA Ops:
  7.2 340.8 %all-gather.2.cloned.1.call-start = ((), (), s32[]{:S(2)}) async-start(), calls=%async_computation | async-start | bytes 10485760 | tf_op jit(solution)/shard_map/all_gather | solution.py:137
  9.5 9.8 %collective-permute-start.1 = (bf16[1,1,1,1,1,8,4096]{6,5,4,3,2,1,0:T(8,128)(2,1)S(1)}, bf16[1,1,1,1,1,8,4096]{6,5,4,3,2,1,0:T(8,128)(2,1)S(1)}, u32[]{:S(2)}, u32[]{:S(2)}) collective-permute-start(bf16[1,1,1,1,1,8,4096]{6,5,4,3,2,1,0:T(8,128)(2,1)S(1)} %maximum_select_fusion.1), channel_id=1, source_target_pairs={{0,32},{2,34},{4,36},{6,38},{8,40},{10,42},{12,44},{14,46},{16,48}... | collective-permute-start | bytes 196616 | tf_op jit(solution)/shard_map/ppermute | solution.py:60
  19.4 8.7 %collective-permute-start.2 = (bf16[2,1,1,1,1,8,4096]{6,5,4,3,2,1,0:T(8,128)(2,1)S(1)}, bf16[2,1,1,1,1,8,4096]{6,5,4,3,2,1,0:T(8,128)(2,1)S(1)}, u32[]{:S(2)}, u32[]{:S(2)}) collective-permute-start(bf16[2,1,1,1,1,8,4096]{6,5,4,3,2,1,0:T(8,128)(2,1)S(1)} %pad_maximum_fusion.10), channel_id=1, source_target_pairs={{0,16},{2,18},{4,20},{6,22},{8,24},{10,26},{12,28},{14,30},{16,0},... | collective-permute-start | bytes 393224 | tf_op jit(solution)/shard_map/ppermute | solution.py:60
  28.2 9.3 %collective-permute-start.3 = (bf16[2,2,1,1,1,8,4096]{6,5,4,3,2,1,0:T(8,128)(2,1)S(1)}, bf16[2,2,1,1,1,8,4096]{6,5,4,3,2,1,0:T(8,128)(2,1)S(1)}, u32[]{:S(2)}, u32[]{:S(2)}) collective-permute-start(bf16[2,2,1,1,1,8,4096]{6,5,4,3,2,1,0:T(8,128)(2,1)S(1)} %pad_maximum_fusion.8), channel_id=1, source_target_pairs={{0,4},{2,6},{4,0},{6,2},{8,12},{10,14},{12,8},{14,10},{16,20},{18,... | collective-permute-start | bytes 786440 | tf_op jit(solution)/shard_map/ppermute | solution.py:60
  37.6 12.6 %collective-permute-start.4 = (bf16[2,2,1,2,1,8,4096]{6,5,4,3,2,1,0:T(8,128)(2,1)S(1)}, bf16[2,2,1,2,1,8,4096]{6,5,4,3,2,1,0:T(8,128)(2,1)}, u32[]{:S(2)}, u32[]{:S(2)}) collective-permute-start(bf16[2,2,1,2,1,8,4096]{6,5,4,3,2,1,0:T(8,128)(2,1)S(1)} %pad_maximum_fusion.6), channel_id=1, source_target_pairs={{0,8},{2,10},{4,12},{6,14},{8,0},{10,2},{12,4},{14,6},{16,24},{18,... | collective-permute-start | bytes 1572872 | tf_op jit(solution)/shard_map/ppermute | solution.py:60
  46.2 39.1 %collective-permute-start.6 = (bf16[2,4096,172]{1,0,2:T(2,128)(2,1)}, bf16[2,4096,172]{1,0,2:T(2,128)(2,1)}, u32[]{:S(2)}, u32[]{:S(2)}) collective-permute-start(bf16[2,4096,172]{1,0,2:T(2,128)(2,1)} %copy.46), channel_id=1, source_target_pairs={{0,1},{1,0},{2,3},{3,2},{4,5},{5,4},{6,7},{7,6},{8,9},{9,8},{10,11... | collective-permute-start | bytes 8454152 | tf_op jit(solution)/shard_map/ppermute | solution.py:117
  52.4 22.9 %collective-permute-start.5 = (bf16[2,2,2,2,1,8,4096]{6,5,4,3,2,1,0:T(8,128)(2,1)}, bf16[2,2,2,2,1,8,4096]{6,5,4,3,2,1,0:T(8,128)(2,1)S(1)}, u32[]{:S(2)}, u32[]{:S(2)}) collective-permute-start(bf16[2,2,2,2,1,8,4096]{6,5,4,3,2,1,0:T(8,128)(2,1)} %pad_maximum_fusion.4), channel_id=1, source_target_pairs={{0,2},{2,0},{4,6},{6,4},{8,10},{10,8},{12,14},{14,12},{16,18},{18,... | collective-permute-start | bytes 3145736 | tf_op jit(solution)/shard_map/ppermute | solution.py:60
  54.5 42.6 %collective-permute-start.7 = (bf16[172,4096]{1,0:T(8,128)(2,1)}, bf16[172,4096]{1,0:T(8,128)(2,1)}, u32[]{:S(2)}, u32[]{:S(2)}) collective-permute-start(bf16[172,4096]{1,0:T(8,128)(2,1)} %broadcast_select_fusion.4), channel_id=1, source_target_pairs={{0,1},{1,0},{2,3},{3,2},{4,5},{5,4},{6,7},{7,6},{8,9},{9,8},{10,11... | collective-permute-start | bytes 4227080 | tf_op jit(solution)/shard_map/ppermute | solution.py:118
  108.6 44.8 %collective-permute-start.8 = (f32[2,2,2,2,1,8,4096]{6,5,4,3,2,1,0:T(8,128)S(1)}, f32[2,2,2,2,1,8,4096]{6,5,4,3,2,1,0:T(8,128)S(1)}, u32[]{:S(2)}, u32[]{:S(2)}) collective-permute-start(f32[2,2,2,2,1,8,4096]{6,5,4,3,2,1,0:T(8,128)S(1)} %slice_select_fusion), channel_id=1, source_target_pairs={{0,2},{2,0},{4,6},{6,4},{8,10},{10,8},{12,14},{14,12},{16,18},{18,... | collective-permute-start | bytes 6291464 | tf_op jit(solution)/shard_map/ppermute | solution.py:77
  153.9 22.3 %collective-permute-start.9 = (f32[2,2,1,2,1,8,4096]{6,5,4,3,2,1,0:T(8,128)S(1)}, f32[2,2,1,2,1,8,4096]{6,5,4,3,2,1,0:T(8,128)S(1)}, u32[]{:S(2)}, u32[]{:S(2)}) collective-permute-start(f32[2,2,1,2,1,8,4096]{6,5,4,3,2,1,0:T(8,128)S(1)} %slice_select_fusion.1), channel_id=1, source_target_pairs={{0,8},{2,10},{4,12},{6,14},{8,0},{10,2},{12,4},{14,6},{16,24},{18,... | collective-permute-start | bytes 3145736 | tf_op jit(solution)/shard_map/ppermute | solution.py:77
  176.6 11.7 %collective-permute-start.10 = (f32[2,2,1,1,1,8,4096]{6,5,4,3,2,1,0:T(8,128)S(1)}, f32[2,2,1,1,1,8,4096]{6,5,4,3,2,1,0:T(8,128)S(1)}, u32[]{:S(2)}, u32[]{:S(2)}) collective-permute-start(f32[2,2,1,1,1,8,4096]{6,5,4,3,2,1,0:T(8,128)S(1)} %slice_select_fusion.2), channel_id=1, source_target_pairs={{0,4},{2,6},{4,0},{6,2},{8,12},{10,14},{12,8},{14,10},{16,20},{18,... | collective-permute-start | bytes 1572872 | tf_op jit(solution)/shard_map/ppermute | solution.py:77
  188.4 12.1 %collective-permute-start.11 = (f32[2,1,1,1,1,8,4096]{6,5,4,3,2,1,0:T(8,128)S(1)}, f32[2,1,1,1,1,8,4096]{6,5,4,3,2,1,0:T(8,128)S(1)}, u32[]{:S(2)}, u32[]{:S(2)}) collective-permute-start(f32[2,1,1,1,1,8,4096]{6,5,4,3,2,1,0:T(8,128)S(1)} %slice_select_fusion.3), channel_id=1, source_target_pairs={{0,16},{2,18},{4,20},{6,22},{8,24},{10,26},{12,28},{14,30},{16,0},... | collective-permute-start | bytes 786440 | tf_op jit(solution)/shard_map/ppermute | solution.py:77
  200.6 9.1 %collective-permute-start.12 = (f32[1,1,1,1,1,8,4096]{6,5,4,3,2,1,0:T(8,128)S(1)}, f32[1,1,1,1,1,8,4096]{6,5,4,3,2,1,0:T(8,128)S(1)}, u32[]{:S(2)}, u32[]{:S(2)}) collective-permute-start(f32[1,1,1,1,1,8,4096]{6,5,4,3,2,1,0:T(8,128)S(1)} %slice_select_fusion.4), channel_id=1, source_target_pairs={{0,32},{2,34},{4,36},{6,38},{8,40},{10,42},{12,44},{14,46},{16,48}... | collective-permute-start | bytes 393224 | tf_op jit(solution)/shard_map/ppermute | solution.py:77
  210.1 8.4 %collective-permute-start.14 = (bf16[1,1,1,1,1,8,4096]{6,5,4,3,2,1,0:T(8,128)(2,1)S(1)}, bf16[1,1,1,1,1,8,4096]{6,5,4,3,2,1,0:T(8,128)(2,1)S(1)}, u32[]{:S(2)}, u32[]{:S(2)}) collective-permute-start(bf16[1,1,1,1,1,8,4096]{6,5,4,3,2,1,0:T(8,128)(2,1)S(1)} %multiply_convert_fusion.2), channel_id=1, source_target_pairs={{0,32},{2,34},{4,36},{6,38},{8,40},{10,42},{12,44},{14,46},{16,48}... | collective-permute-start | bytes 196616 | tf_op jit(solution)/shard_map/ppermute | solution.py:60
  218.5 7.4 %collective-permute-start.15 = (bf16[2,1,1,1,1,8,4096]{6,5,4,3,2,1,0:T(8,128)(2,1)S(1)}, bf16[2,1,1,1,1,8,4096]{6,5,4,3,2,1,0:T(8,128)(2,1)S(1)}, u32[]{:S(2)}, u32[]{:S(2)}) collective-permute-start(bf16[2,1,1,1,1,8,4096]{6,5,4,3,2,1,0:T(8,128)(2,1)S(1)} %pad_maximum_fusion.11), channel_id=1, source_target_pairs={{0,16},{2,18},{4,20},{6,22},{8,24},{10,26},{12,28},{14,30},{16,0},... | collective-permute-start | bytes 393224 | tf_op jit(solution)/shard_map/ppermute | solution.py:60
  225.9 8.0 %collective-permute-start.16 = (bf16[2,2,1,1,1,8,4096]{6,5,4,3,2,1,0:T(8,128)(2,1)S(1)}, bf16[2,2,1,1,1,8,4096]{6,5,4,3,2,1,0:T(8,128)(2,1)S(1)}, u32[]{:S(2)}, u32[]{:S(2)}) collective-permute-start(bf16[2,2,1,1,1,8,4096]{6,5,4,3,2,1,0:T(8,128)(2,1)S(1)} %pad_maximum_fusion.9), channel_id=1, source_target_pairs={{0,4},{2,6},{4,0},{6,2},{8,12},{10,14},{12,8},{14,10},{16,20},{18,... | collective-permute-start | bytes 786440 | tf_op jit(solution)/shard_map/ppermute | solution.py:60
  233.9 9.3 %collective-permute-start.17 = (bf16[2,2,1,2,1,8,4096]{6,5,4,3,2,1,0:T(8,128)(2,1)S(1)}, bf16[2,2,1,2,1,8,4096]{6,5,4,3,2,1,0:T(8,128)(2,1)S(1)}, u32[]{:S(2)}, u32[]{:S(2)}) collective-permute-start(bf16[2,2,1,2,1,8,4096]{6,5,4,3,2,1,0:T(8,128)(2,1)S(1)} %pad_maximum_fusion.7), channel_id=1, source_target_pairs={{0,8},{2,10},{4,12},{6,14},{8,0},{10,2},{12,4},{14,6},{16,24},{18,... | collective-permute-start | bytes 1572872 | tf_op jit(solution)/shard_map/ppermute | solution.py:60
  243.4 18.5 %collective-permute-start.18 = (bf16[2,2,2,2,1,8,4096]{6,5,4,3,2,1,0:T(8,128)(2,1)S(1)}, bf16[2,2,2,2,1,8,4096]{6,5,4,3,2,1,0:T(8,128)(2,1)S(1)}, u32[]{:S(2)}, u32[]{:S(2)}) collective-permute-start(bf16[2,2,2,2,1,8,4096]{6,5,4,3,2,1,0:T(8,128)(2,1)S(1)} %pad_maximum_fusion.5), channel_id=1, source_target_pairs={{0,2},{2,0},{4,6},{6,4},{8,10},{10,8},{12,14},{14,12},{16,18},{18,... | collective-permute-start | bytes 3145736 | tf_op jit(solution)/shard_map/ppermute | solution.py:60
  269.0 4.7 %collective-permute-start.19 = (bf16[250,4096]{1,0:T(8,128)(2,1)}, bf16[250,4096]{1,0:T(8,128)(2,1)}, u32[]{:S(2)}, u32[]{:S(2)}) collective-permute-start(bf16[250,4096]{1,0:T(8,128)(2,1)} %get-tuple-element.23), channel_id=1, source_target_pairs={{0,1},{1,0},{2,3},{3,2},{4,5},{5,4},{6,7},{7,6},{8,9},{9,8},{10,11... | collective-permute-start | bytes 6144008 | tf_op jit(solution)/shard_map/ppermute | solution.py:139
  362.1 5.4 %collective-permute-start.22 = (f32[2,3,1024]{2,0,1:T(2,128)S(1)}, f32[2,3,1024]{2,0,1:T(2,128)S(1)}, u32[]{:S(2)}, u32[]{:S(2)}) collective-permute-start(f32[2,3,1024]{2,0,1:T(2,128)S(1)} %pad_maximum_fusion.12), channel_id=1, source_target_pairs={{0,4},{2,6},{4,0},{6,2},{8,12},{10,14},{12,8},{14,10},{16,20},{18,... | collective-permute-start | bytes 73736 | tf_op jit(solution)/shard_map/ppermute | solution.py:155
  371.6 4.8 %collective-permute-start.24 = (f32[2,3,1024]{2,0,1:T(2,128)S(1)}, f32[2,3,1024]{2,0,1:T(2,128)S(1)}, u32[]{:S(2)}, u32[]{:S(2)}) collective-permute-start(f32[2,3,1024]{2,0,1:T(2,128)S(1)} %pad_maximum_fusion.14), channel_id=1, source_target_pairs={{0,16},{2,18},{4,20},{6,22},{8,24},{10,26},{12,28},{14,30},{16,0},... | collective-permute-start | bytes 73736 | tf_op jit(solution)/shard_map/ppermute | solution.py:155
  376.5 7.8 %collective-permute-start.25 = (f32[2,3,1024]{2,0,1:T(2,128)S(1)}, f32[2,3,1024]{2,0,1:T(2,128)S(1)}, u32[]{:S(2)}, u32[]{:S(2)}) collective-permute-start(f32[2,3,1024]{2,0,1:T(2,128)S(1)} %pad_maximum_fusion.15), channel_id=1, source_target_pairs={{0,32},{2,34},{4,36},{6,38},{8,40},{10,42},{12,44},{14,46},{16,48}... | collective-permute-start | bytes 73736 | tf_op jit(solution)/shard_map/ppermute | solution.py:155
  385.9 5.2 %collective-permute-start.13 = (bf16[4,4096]{1,0:T(4,128)(2,1)S(1)}, bf16[4,4096]{1,0:T(4,128)(2,1)S(1)}, u32[]{:S(2)}, u32[]{:S(2)}) collective-permute-start(bf16[4,4096]{1,0:T(4,128)(2,1)S(1)} %constant_dynamic-slice_fusion), channel_id=1, source_target_pairs={{0,1},{1,0},{2,3},{3,2},{4,5},{5,4},{6,7},{7,6},{8,9},{9,8},{10,11... | collective-permute-start | bytes 98312 | tf_op jit(solution)/shard_map/ppermute | solution.py:133
  388.4 5.4 %collective-permute-start.27 = (f32[2,3,1024]{2,0,1:T(2,128)S(1)}, f32[2,3,1024]{2,0,1:T(2,128)S(1)}, u32[]{:S(2)}, u32[]{:S(2)}) collective-permute-start(f32[2,3,1024]{2,0,1:T(2,128)S(1)} %pad_maximum_fusion.17), channel_id=1, source_target_pairs={{0,128},{64,192},{128,0},{192,64},{1,129},{65,193},{129,1},{193,65... | collective-permute-start | bytes 73736 | tf_op jit(solution)/shard_map/ppermute | solution.py:155
  (24 other events, 342.3 us)
Sparse Core Ops, SparseCore 0:
  263.7 84.2 all-gather.1

commit v5 on v3

--- a/solution.py
+++ b/solution.py
@@ -42,6 +42,63 @@
         jnp.float32
     )
     return jnp.sum(log_ratio[:, None] * onehot, axis=0)
+
+
+def zx_bits():
+    size = lax.axis_size("zx")
+    return [1 << k for k in reversed(range(size.bit_length() - 1))]
+
+
+def gather_doubling(block, orders=((16, 8, 2, 4, 1), (16, 2, 8, 1, 4))):
+    bits = zx_bits()
+    spot = lax.axis_index("zx")
+    size = lax.axis_size("zx")
+    width = block.shape[-1] // len(orders)
+    parts = []
+    for k in range(len(orders)):
+        piece = lax.slice_in_dim(block, k * width, (k + 1) * width, axis=block.ndim - 1)
+        parts.append(piece.reshape((1,) * len(bits) + piece.shape))
+    for step in range(len(orders[0])):
+        for k, order in enumerate(orders):
+            bit = order[step]
+            if bit not in bits:
+                continue
+            dim = bits.index(bit)
+            held = parts[k]
+            other = lax.ppermute(held, "zx", [(i, i ^ bit) for i in range(size)])
+            low = (spot & bit) == 0
+            parts[k] = jnp.concatenate(
+                [jnp.where(low, held, other), jnp.where(low, other, held)], axis=dim
+            )
+    rows = [p.reshape((-1,) + p.shape[len(bits) + 1 :]) for p in parts]
+    return jnp.concatenate(rows, axis=-1)
+
+
+def scatter_halving(full, orders=((1, 4, 2, 8, 16), (4, 1, 8, 2, 16))):
+    bits = zx_bits()
+    spot = lax.axis_index("zx")
+    size = lax.axis_size("zx")
+    width = full.shape[-1] // len(orders)
+    parts = []
+    for k in range(len(orders)):
+        piece = lax.slice_in_dim(full, k * width, (k + 1) * width, axis=full.ndim - 1)
+        parts.append(piece.reshape((2,) * len(bits) + (-1,) + piece.shape[1:]))
+    for step in range(len(orders[0])):
+        for k, order in enumerate(orders):
+            bit = order[step]
+            if bit not in bits:
+                continue
+            dim = bits.index(bit)
+            held = parts[k]
+            lower = lax.slice_in_dim(held, 0, 1, axis=dim)
+            upper = lax.slice_in_dim(held, 1, 2, axis=dim)
+            low = (spot & bit) == 0
+            other = lax.ppermute(
+                jnp.where(low, upper, lower), "zx", [(i, i ^ bit) for i in range(size)]
+            )
+            parts[k] = jnp.where(low, lower, upper) + other
+    rows = [p.reshape((-1,) + full.shape[1:-1] + (width,)) for p in parts]
+    return jnp.concatenate(rows, axis=-1)
 
 
 def pick(first, pol, ref):
@@ -84,16 +141,16 @@
     pair_rows = jnp.where(
         first, jnp.concatenate([keep_h, got_h]), jnp.concatenate([got_h, keep_h])
     )
-    group_rows = lax.all_gather(pair_rows, "zx", axis=0, tiled=True)
+    group_rows = gather_doubling(pair_rows)
     mlp_gain = jnp.where(first, pol_mlp_gain, ref_mlp_gain)
     partial = mlp_partial(group_rows, mlp_gain, keep_w[0], keep_w[1], keep_d) + mlp_partial(
         group_rows, mlp_gain, got_w[0], got_w[1], got_d
     )
-    mixed = lax.psum(partial, "zx")
-    out = (group_rows.astype(jnp.float32) + mixed).astype(jnp.bfloat16)
-    final = rms_rows(out, jnp.where(first, pol_final_gain, ref_final_gain))
-    mine_out = lax.dynamic_slice_in_dim(out, member * rows, rows, axis=0)
-    sent_out = lax.ppermute(lax.dynamic_slice_in_dim(out, partner * rows, rows, axis=0), "core", SWAP)
+    mixed = scatter_halving(partial)
+    out = (pair_rows.astype(jnp.float32) + mixed).astype(jnp.bfloat16)
+    final = gather_doubling(rms_rows(out, jnp.where(first, pol_final_gain, ref_final_gain)))
+    mine_out = lax.dynamic_slice_in_dim(out, core * rows, rows, axis=0)
+    sent_out = lax.ppermute(lax.dynamic_slice_in_dim(out, (1 - core) * rows, rows, axis=0), "core", SWAP)
     pol_out = jnp.where(first, mine_out, sent_out)
     ref_out = jnp.where(first, sent_out, mine_out)
 

time: 419 us -> 362 us (0.86)
  waiting for transfers between devices: 319 us -> 205 us
  starting transfers between devices: 17.9 us -> 67.7 us
  matrix products: 28.6 us -> 35.6 us
    psum x1 -> x0, waiting for transfers between devices: 161 us -> none  [per_device(): mixed = lax.psum(partial, 'zx')]
    ppermute x1 -> x31, waiting for transfers between devices: 0.01 us -> 109 us  [the longest x20 68.9 us: gather_doubling(): other = lax.ppermute(held, 'zx', [(i, i ^ bit) for i in range(size)])]
    all_gather x1 -> x0, waiting for transfers between devices: 58.3 us -> none  [per_device(): group_rows = lax.all_gather(pair_rows, 'zx', axis=0, tiled=True)]
    ppermute x1 -> x31, starting transfers between devices: 0.09 us -> 50.2 us  [the longest x20 27.2 us: gather_doubling(): other = lax.ppermute(held, 'zx', [(i, i ^ bit) for i in range(size)])]
    dot_general x2, matrix products: 14.8 us -> 24.5 us  [mlp_partial(): return jnp.dot(hidden, w_down, preferred_element_type=jnp.float32)]
    reduce_sum x2, other arithmetic: 5.25 us -> 0.65 us  [rms_rows(): scale = lax.rsqrt(jnp.mean(values * values, axis=-1, keepdims=True) + 1e-05)]
  transfers between devices with their start and end apart: 16 -> 44, of which waited for: 14 -> 36; matrix products, arithmetic and copies ran while one was open for 9% -> 9% of each run, Pallas kernels for 0% -> 0%
where the time goes in v5:
time: 362 us; the launch traced here: 358 us
  waiting for transfers between devices  205 us (57%)
  starting transfers between devices  67.7 us (19%)
  matrix products  35.6 us (10%)
  other arithmetic  18.2 us (5%)
  local copies, waits for them, and re-layouts  15.9 us (4%)
  between operations  15.1 us (4%)
    all_gather x1, waiting for transfers between devices, per_device(): every = lax.all_gather(final, 'grp', axis=0, tiled=True)  73.7 us
    ppermute x20, waiting for transfers between devices, gather_doubling(): other = lax.ppermute(held, 'zx', [(i, i ^ bit) for i in range(size)])  68.9 us
    ppermute x10, waiting for transfers between devices, scatter_halving(): lax.ppermute(jnp.where(low, upper, lower), 'zx', [(i, i ^ bit) for i in r...  39.7 us
    ppermute x20, starting transfers between devices, gather_doubling(): other = lax.ppermute(held, 'zx', [(i, i ^ bit) for i in range(size)])  27.2 us
    dot_general x2, matrix products, mlp_partial(): return jnp.dot(hidden, w_down, preferred_element_type=jnp.float32)  24.5 us
    ppermute x10, starting transfers between devices, scatter_halving(): lax.ppermute(jnp.where(low, upper, lower), 'zx', [(i, i ^ bit) for i in r...  22.9 us
    ppermute x7, waiting for transfers between devices, per_device(): other = lax.ppermute(state, axis, [(i, i ^ bit) for i in range(size)])  17.2 us
    ppermute x7, starting transfers between devices, per_device(): other = lax.ppermute(state, axis, [(i, i ^ bit) for i in range(size)])  16.9 us
  transfers between devices with their start and end apart: 44, of which 36 were waited for; matrix products, arithmetic and copies ran while one was open for 9% of the time, Pallas kernels for 0%

profile of v5, /device:TPU:6, one launch (start us, length us, event | category | flops | bytes accessed | tf_op | source)
XLA Modules:
  0.0 357.7 jit_solution(820397544745581586)
XLA Ops:
  8.1 4.5 %broadcast_select_fusion = (bf16[2,4096,172]{1,2,0:T(8,128)(2,1)S(1)}, bf16[2,4096,172]{1,2,0:T(8,128)(2,1)}) fusion(pred[]{:T(512)S(6)} %eq.28, bf16[1,4096,172]{1,2,0:T(8,128)(2,1)} %bitcast.111, bf16[1,4096,172]{1,2,0:T(8,128)(2,1)} %bitcast.112, bf16[1,4096,172]{1,2,0:T(8,128)(2,1)} %bitcast.113, bf16[1,4096,172]{1,2,0:T(8,128)(2,1)} %bitcast.114), kind=kLoop, calls=%fused_computation.12 | loop fusion | flops 5636096 | bytes 11272193 | tf_op jit(solution)/shard_map/jit(_where)/select_n | solution.py:105
  12.6 4.6 %copy.46 = bf16[2,4096,172]{1,0,2:T(2,128)(2,1)} copy(bf16[2,4096,172]{1,2,0:T(8,128)(2,1)S(1)} %get-tuple-element.19) | data formatting | bytes 5636096 | tf_op jit(solution)/shard_map/jit(_where)/select_n | solution.py:105
  17.8 7.3 %collective-permute-start.1 = (bf16[1,1,1,1,1,8,2048]{6,5,4,3,2,1,0:T(8,128)(2,1)S(1)}, bf16[1,1,1,1,1,8,2048]{6,5,4,3,2,1,0:T(8,128)(2,1)S(1)}, u32[]{:S(2)}, u32[]{:S(2)}) collective-permute-start(bf16[1,1,1,1,1,8,2048]{6,5,4,3,2,1,0:T(8,128)(2,1)S(1)} %get-tuple-element.75), channel_id=1, source_target_pairs={{0,32},{2,34},{4,36},{6,38},{8,40},{10,42},{12,44},{14,46},{16,48}... | collective-permute-start | bytes 98312 | tf_op jit(solution)/shard_map/ppermute | solution.py:68
  27.0 6.3 %collective-permute-done.6 = bf16[1,1,1,1,1,8,2048]{6,5,4,3,2,1,0:T(8,128)(2,1)S(1)} collective-permute-done((bf16[1,1,1,1,1,8,2048]{6,5,4,3,2,1,0:T(8,128)(2,1)S(1)}, bf16[1,1,1,1,1,8,2048]{6,5,4,3,2,1,0:T(8,128)(2,1)S(1)}, u32[]{:S(2)}, u32[]{:S(2)}) %collective-permute-start.6) | collective-permute-done | bytes 32800 | tf_op jit(solution)/shard_map/ppermute | solution.py:68
  49.7 4.0 %collective-permute-done.4 = bf16[2,2,1,2,1,8,2048]{6,5,4,3,2,1,0:T(8,128)(2,1)S(1)} collective-permute-done((bf16[2,2,1,2,1,8,2048]{6,5,4,3,2,1,0:T(8,128)(2,1)S(1)}, bf16[2,2,1,2,1,8,2048]{6,5,4,3,2,1,0:T(8,128)(2,1)S(1)}, u32[]{:S(2)}, u32[]{:S(2)}) %collective-permute-start.4) | collective-permute-done | bytes 262176 | tf_op jit(solution)/shard_map/ppermute | solution.py:68
  59.9 6.7 %collective-permute-done.5 = bf16[2,2,2,2,1,8,2048]{6,5,4,3,2,1,0:T(8,128)(2,1)S(1)} collective-permute-done((bf16[2,2,2,2,1,8,2048]{6,5,4,3,2,1,0:T(8,128)(2,1)S(1)}, bf16[2,2,2,2,1,8,2048]{6,5,4,3,2,1,0:T(8,128)(2,1)S(1)}, u32[]{:S(2)}, u32[]{:S(2)}) %collective-permute-start.5) | collective-permute-done | bytes 524320 | tf_op jit(solution)/shard_map/ppermute | solution.py:68
  71.3 7.1 %fusion.11 = f32[256,4096]{1,0:T(8,128)} fusion(bf16[172,4096]{1,0:T(8,128)(2,1)} %param.24, bf16[172,4096]{1,0:T(8,128)(2,1)} %param.27, pred[]{:T(512)S(6)} %eq.28, bf16[2,4096,172]{1,2,0:T(8,128)(2,1)} %get-tuple-element.20, f32[256,172]{0,1:T(8,128)S(1)} %fusion.8, f32[4096]{0:T(1024)S(1)} %select_convert_fusion.1, f32[256]{0:T(256)S(1)} %add_rsqrt_fusion, ...), kind=kOutput, calls=%fused_computation.28 | convolution fusion | flops 729729024 | bytes 10810369 | tf_op jit(solution)/shard_map/dot_general | solution.py:21
  78.4 5.5 %fusion.51 = (bf16[1,4096,172]{1,0,2:T(2,128)(2,1)}, bf16[1,4096,172]{1,0,2:T(2,128)(2,1)S(1)}) fusion(bf16[2,4096,172]{1,0,2:T(2,128)(2,1)S(1)} %collective-permute-done.11), kind=kLoop, calls=%fused_computation.220 | loop fusion | bytes 5636096 | tf_op jit(solution)/shard_map/slice | solution.py:147
  85.9 17.4 %convolution_add_fusion = f32[256,4096]{1,0:T(8,128)} fusion(f32[256,4096]{1,0:T(8,128)} %fusion.11, bf16[172,4096]{1,0:T(8,128)(2,1)} %collective-permute-done.12, f32[256,172]{0,1:T(8,128)S(1)} %fusion.9, bf16[1,4096,172]{1,0,2:T(2,128)(2,1)} %get-tuple-element.25, f32[4096]{0:T(1024)S(1)} %select_convert_fusion.1, f32[256]{0:T(256)S(1)} %add_rsqrt_fusion, ...), kind=kOutput, calls=%fused_computation | convolution fusion | flops 730073088 | bytes 13497344 | tf_op jit(solution)/shard_map/dot_general | solution.py:21
  107.2 19.8 %collective-permute-done.13 = f32[2,2,2,2,1,8,2048]{6,5,4,3,2,1,0:T(8,128)S(1)} collective-permute-done((f32[2,2,2,2,1,8,2048]{6,5,4,3,2,1,0:T(8,128)S(1)}, f32[2,2,2,2,1,8,2048]{6,5,4,3,2,1,0:T(8,128)S(1)}, u32[]{:S(2)}, u32[]{:S(2)}) %collective-permute-start.13) | collective-permute-done | bytes 1048608 | tf_op jit(solution)/shard_map/ppermute | solution.py:96
  131.6 7.9 %collective-permute-done.14 = f32[2,2,1,2,1,8,2048]{6,5,4,3,2,1,0:T(8,128)S(1)} collective-permute-done((f32[2,2,1,2,1,8,2048]{6,5,4,3,2,1,0:T(8,128)S(1)}, f32[2,2,1,2,1,8,2048]{6,5,4,3,2,1,0:T(8,128)S(1)}, u32[]{:S(2)}, u32[]{:S(2)}) %collective-permute-start.14) | collective-permute-done | bytes 524320 | tf_op jit(solution)/shard_map/ppermute | solution.py:96
  143.1 4.8 %collective-permute-done.15 = f32[2,2,1,1,1,8,2048]{6,5,4,3,2,1,0:T(8,128)S(1)} collective-permute-done((f32[2,2,1,1,1,8,2048]{6,5,4,3,2,1,0:T(8,128)S(1)}, f32[2,2,1,1,1,8,2048]{6,5,4,3,2,1,0:T(8,128)S(1)}, u32[]{:S(2)}, u32[]{:S(2)}) %collective-permute-start.15) | collective-permute-done | bytes 262176 | tf_op jit(solution)/shard_map/ppermute | solution.py:96
  153.2 5.3 %collective-permute-start.21 = (f32[2,1,1,1,1,8,2048]{6,5,4,3,2,1,0:T(8,128)S(1)}, f32[2,1,1,1,1,8,2048]{6,5,4,3,2,1,0:T(8,128)S(1)}, u32[]{:S(2)}, u32[]{:S(2)}) collective-permute-start(f32[2,1,1,1,1,8,2048]{6,5,4,3,2,1,0:T(8,128)S(1)} %slice_select_fusion.6), channel_id=1, source_target_pairs={{0,4},{2,6},{4,0},{6,2},{8,12},{10,14},{12,8},{14,10},{16,20},{18,... | collective-permute-start | bytes 393224 | tf_op jit(solution)/shard_map/ppermute | solution.py:96
  161.5 5.1 %collective-permute-start.22 = (f32[1,1,1,1,1,8,2048]{6,5,4,3,2,1,0:T(8,128)S(1)}, f32[1,1,1,1,1,8,2048]{6,5,4,3,2,1,0:T(8,128)S(1)}, u32[]{:S(2)}, u32[]{:S(2)}) collective-permute-start(f32[1,1,1,1,1,8,2048]{6,5,4,3,2,1,0:T(8,128)S(1)} %slice_select_fusion.8), channel_id=1, source_target_pairs={{0,32},{2,34},{4,36},{6,38},{8,40},{10,42},{12,44},{14,46},{16,48}... | collective-permute-start | bytes 196616 | tf_op jit(solution)/shard_map/ppermute | solution.py:96
  170.1 5.2 %collective-permute-start.24 = (bf16[1,1,1,1,1,8,2048]{6,5,4,3,2,1,0:T(8,128)(2,1)S(1)}, bf16[1,1,1,1,1,8,2048]{6,5,4,3,2,1,0:T(8,128)(2,1)S(1)}, u32[]{:S(2)}, u32[]{:S(2)}) collective-permute-start(bf16[1,1,1,1,1,8,2048]{6,5,4,3,2,1,0:T(8,128)(2,1)S(1)} %get-tuple-element.71), channel_id=1, source_target_pairs={{0,32},{2,34},{4,36},{6,38},{8,40},{10,42},{12,44},{14,46},{16,48}... | collective-permute-start | bytes 98312 | tf_op jit(solution)/shard_map/ppermute | solution.py:68
  178.0 5.2 %collective-permute-done.29 = bf16[1,1,1,1,1,8,2048]{6,5,4,3,2,1,0:T(8,128)(2,1)S(1)} collective-permute-done((bf16[1,1,1,1,1,8,2048]{6,5,4,3,2,1,0:T(8,128)(2,1)S(1)}, bf16[1,1,1,1,1,8,2048]{6,5,4,3,2,1,0:T(8,128)(2,1)S(1)}, u32[]{:S(2)}, u32[]{:S(2)}) %collective-permute-start.29) | collective-permute-done | bytes 32800 | tf_op jit(solution)/shard_map/ppermute | solution.py:68
  183.4 7.1 %collective-permute-done.25 = bf16[2,1,1,1,1,8,2048]{6,5,4,3,2,1,0:T(8,128)(2,1)S(1)} collective-permute-done((bf16[2,1,1,1,1,8,2048]{6,5,4,3,2,1,0:T(8,128)(2,1)S(1)}, bf16[2,1,1,1,1,8,2048]{6,5,4,3,2,1,0:T(8,128)(2,1)S(1)}, u32[]{:S(2)}, u32[]{:S(2)}) %collective-permute-start.25) | collective-permute-done | bytes 65568 | tf_op jit(solution)/shard_map/ppermute | solution.py:68
  192.2 6.4 %collective-permute-done.26 = bf16[2,2,1,1,1,8,2048]{6,5,4,3,2,1,0:T(8,128)(2,1)S(1)} collective-permute-done((bf16[2,2,1,1,1,8,2048]{6,5,4,3,2,1,0:T(8,128)(2,1)S(1)}, bf16[2,2,1,1,1,8,2048]{6,5,4,3,2,1,0:T(8,128)(2,1)S(1)}, u32[]{:S(2)}, u32[]{:S(2)}) %collective-permute-start.26) | collective-permute-done | bytes 131104 | tf_op jit(solution)/shard_map/ppermute | solution.py:68
  200.1 7.9 %collective-permute-done.27 = bf16[2,2,1,2,1,8,2048]{6,5,4,3,2,1,0:T(8,128)(2,1)S(1)} collective-permute-done((bf16[2,2,1,2,1,8,2048]{6,5,4,3,2,1,0:T(8,128)(2,1)S(1)}, bf16[2,2,1,2,1,8,2048]{6,5,4,3,2,1,0:T(8,128)(2,1)S(1)}, u32[]{:S(2)}, u32[]{:S(2)}) %collective-permute-start.27) | collective-permute-done | bytes 262176 | tf_op jit(solution)/shard_map/ppermute | solution.py:68
  209.3 8.0 %collective-permute-done.28 = bf16[2,2,2,2,1,8,2048]{6,5,4,3,2,1,0:T(8,128)(2,1)S(1)} collective-permute-done((bf16[2,2,2,2,1,8,2048]{6,5,4,3,2,1,0:T(8,128)(2,1)S(1)}, bf16[2,2,2,2,1,8,2048]{6,5,4,3,2,1,0:T(8,128)(2,1)S(1)}, u32[]{:S(2)}, u32[]{:S(2)}) %collective-permute-start.28) | collective-permute-done | bytes 524320 | tf_op jit(solution)/shard_map/ppermute | solution.py:68
  225.8 4.4 %collective-permute-done.34 = bf16[250,4096]{1,0:T(8,128)(2,1)} collective-permute-done((bf16[250,4096]{1,0:T(8,128)(2,1)}, bf16[250,4096]{1,0:T(8,128)(2,1)}, u32[]{:S(2)}, u32[]{:S(2)}) %collective-permute-start.34) | collective-permute-done | bytes 2048032 | tf_op jit(solution)/shard_map/ppermute | solution.py:159
  230.3 73.7 %all-gather.2.cloned.1.call-done = bf16[1024,4096]{1,0:T(8,128)(2,1)} async-done(((bf16[256,4096]{1,0:T(8,128)(2,1)}), bf16[1024,4096]{1,0:T(8,128)(2,1)}) %all-gather.2.cloned.1.call-update) | async-done | bytes 8388624 | tf_op jit(solution)/shard_map/all_gather | solution.py:157
  304.0 8.2 %fusion.53 = (f32[1024]{0:T(1024)S(1)}, f32[1024,500]{0,1:T(8,128)S(1)}) fusion(bf16[1024,4096]{1,0:T(8,128)(2,1)} %all-gather.2.cloned.1.call-done, bf16[250,4096]{1,0:T(8,128)(2,1)} %collective-permute-done.34, bf16[250,4096]{1,0:T(8,128)(2,1)} %get-tuple-element.21), kind=kOutput, calls=%fused_computation.222 | convolution fusion | flops 4203006976 | bytes 14536704 | tf_op jit(solution)/shard_map/td,vd->tv/dot_general | solution.py:25
  332.5 5.8 %collective-permute-start.40 = (f32[2,3,1024]{2,0,1:T(2,128)S(1)}, f32[2,3,1024]{2,0,1:T(2,128)S(1)}, u32[]{:S(2)}, u32[]{:S(2)}) collective-permute-start(f32[2,3,1024]{2,0,1:T(2,128)S(1)} %pad_maximum_fusion.27), channel_id=1, source_target_pairs={{0,32},{2,34},{4,36},{6,38},{8,40},{10,42},{12,44},{14,46},{16,48}... | collective-permute-start | bytes 73736 | tf_op jit(solution)/shard_map/ppermute | solution.py:175
  (214 shorter events, 104.3 us)
Async XLA Ops:
  7.2 296.8 %all-gather.2.cloned.1.call-start = ((), (), s32[]{:S(2)}) async-start(), calls=%async_computation | async-start | bytes 10485760 | tf_op jit(solution)/shard_map/all_gather | solution.py:157
  8.0 9.7 %collective-permute-start = (bf16[4,4096]{1,0:T(4,128)(2,1)S(1)}, bf16[4,4096]{1,0:T(4,128)(2,1)S(1)}, u32[]{:S(2)}, u32[]{:S(2)}) collective-permute-start(bf16[4,4096]{1,0:T(4,128)(2,1)S(1)} %get-tuple-element.78), channel_id=1, source_target_pairs={{0,1},{1,0},{2,3},{3,2},{4,5},{5,4},{6,7},{7,6},{8,9},{9,8},{10,11... | collective-permute-start | bytes 98312 | tf_op jit(solution)/shard_map/ppermute | solution.py:140
  17.2 61.2 %collective-permute-start.11 = (bf16[2,4096,172]{1,0,2:T(2,128)(2,1)}, bf16[2,4096,172]{1,0,2:T(2,128)(2,1)S(1)}, u32[]{:S(2)}, u32[]{:S(2)}) collective-permute-start(bf16[2,4096,172]{1,0,2:T(2,128)(2,1)} %copy.46), channel_id=1, source_target_pairs={{0,1},{1,0},{2,3},{3,2},{4,5},{5,4},{6,7},{7,6},{8,9},{9,8},{10,11... | collective-permute-start | bytes 8454152 | tf_op jit(solution)/shard_map/ppermute | solution.py:137
  17.8 9.2 %collective-permute-start.1 = (bf16[1,1,1,1,1,8,2048]{6,5,4,3,2,1,0:T(8,128)(2,1)S(1)}, bf16[1,1,1,1,1,8,2048]{6,5,4,3,2,1,0:T(8,128)(2,1)S(1)}, u32[]{:S(2)}, u32[]{:S(2)}) collective-permute-start(bf16[1,1,1,1,1,8,2048]{6,5,4,3,2,1,0:T(8,128)(2,1)S(1)} %get-tuple-element.75), channel_id=1, source_target_pairs={{0,32},{2,34},{4,36},{6,38},{8,40},{10,42},{12,44},{14,46},{16,48}... | collective-permute-start | bytes 98312 | tf_op jit(solution)/shard_map/ppermute | solution.py:68
  25.1 8.2 %collective-permute-start.6 = (bf16[1,1,1,1,1,8,2048]{6,5,4,3,2,1,0:T(8,128)(2,1)S(1)}, bf16[1,1,1,1,1,8,2048]{6,5,4,3,2,1,0:T(8,128)(2,1)S(1)}, u32[]{:S(2)}, u32[]{:S(2)}) collective-permute-start(bf16[1,1,1,1,1,8,2048]{6,5,4,3,2,1,0:T(8,128)(2,1)S(1)} %get-tuple-element.76), channel_id=1, source_target_pairs={{0,32},{2,34},{4,36},{6,38},{8,40},{10,42},{12,44},{14,46},{16,48}... | collective-permute-start | bytes 98312 | tf_op jit(solution)/shard_map/ppermute | solution.py:68
  26.5 59.3 %collective-permute-start.12 = (bf16[172,4096]{1,0:T(8,128)(2,1)}, bf16[172,4096]{1,0:T(8,128)(2,1)}, u32[]{:S(2)}, u32[]{:S(2)}) collective-permute-start(bf16[172,4096]{1,0:T(8,128)(2,1)} %broadcast_select_fusion.4), channel_id=1, source_target_pairs={{0,1},{1,0},{2,3},{3,2},{4,5},{5,4},{6,7},{7,6},{8,9},{9,8},{10,11... | collective-permute-start | bytes 4227080 | tf_op jit(solution)/shard_map/ppermute | solution.py:138
  49.3 9.2 %collective-permute-start.9 = (bf16[2,2,1,2,1,8,2048]{6,5,4,3,2,1,0:T(8,128)(2,1)S(1)}, bf16[2,2,1,2,1,8,2048]{6,5,4,3,2,1,0:T(8,128)(2,1)S(1)}, u32[]{:S(2)}, u32[]{:S(2)}) collective-permute-start(bf16[2,2,1,2,1,8,2048]{6,5,4,3,2,1,0:T(8,128)(2,1)S(1)} %pad_maximum_fusion.13), channel_id=1, source_target_pairs={{0,2},{2,0},{4,6},{6,4},{8,10},{10,8},{12,14},{14,12},{16,18},{18,... | collective-permute-start | bytes 786440 | tf_op jit(solution)/shard_map/ppermute | solution.py:68
  53.9 12.7 %collective-permute-start.5 = (bf16[2,2,2,2,1,8,2048]{6,5,4,3,2,1,0:T(8,128)(2,1)S(1)}, bf16[2,2,2,2,1,8,2048]{6,5,4,3,2,1,0:T(8,128)(2,1)S(1)}, u32[]{:S(2)}, u32[]{:S(2)}) collective-permute-start(bf16[2,2,2,2,1,8,2048]{6,5,4,3,2,1,0:T(8,128)(2,1)S(1)} %pad_maximum_fusion.8), channel_id=1, source_target_pairs={{0,2},{2,0},{4,6},{6,4},{8,10},{10,8},{12,14},{14,12},{16,18},{18,... | collective-permute-start | bytes 1572872 | tf_op jit(solution)/shard_map/ppermute | solution.py:68
  58.6 9.5 %collective-permute-start.10 = (bf16[2,2,1,2,2,8,2048]{6,5,4,3,2,1,0:T(8,128)(2,1)S(1)}, bf16[2,2,1,2,2,8,2048]{6,5,4,3,2,1,0:T(8,128)(2,1)S(1)}, u32[]{:S(2)}, u32[]{:S(2)}) collective-permute-start(bf16[2,2,1,2,2,8,2048]{6,5,4,3,2,1,0:T(8,128)(2,1)S(1)} %pad_maximum_fusion.9), channel_id=1, source_target_pairs={{0,8},{2,10},{4,12},{6,14},{8,0},{10,2},{12,4},{14,6},{16,24},{18,... | collective-permute-start | bytes 1572872 | tf_op jit(solution)/shard_map/ppermute | solution.py:68
  106.0 21.1 %collective-permute-start.13 = (f32[2,2,2,2,1,8,2048]{6,5,4,3,2,1,0:T(8,128)S(1)}, f32[2,2,2,2,1,8,2048]{6,5,4,3,2,1,0:T(8,128)S(1)}, u32[]{:S(2)}, u32[]{:S(2)}) collective-permute-start(f32[2,2,2,2,1,8,2048]{6,5,4,3,2,1,0:T(8,128)S(1)} %slice_select_fusion.1), channel_id=1, source_target_pairs={{0,2},{2,0},{4,6},{6,4},{8,10},{10,8},{12,14},{14,12},{16,18},{18,... | collective-permute-start | bytes 3145736 | tf_op jit(solution)/shard_map/ppermute | solution.py:96
  106.4 23.6 %collective-permute-start.18 = (f32[2,2,1,2,2,8,2048]{6,5,4,3,2,1,0:T(8,128)S(1)}, f32[2,2,1,2,2,8,2048]{6,5,4,3,2,1,0:T(8,128)S(1)}, u32[]{:S(2)}, u32[]{:S(2)}) collective-permute-start(f32[2,2,1,2,2,8,2048]{6,5,4,3,2,1,0:T(8,128)S(1)} %slice_select_fusion), channel_id=1, source_target_pairs={{0,8},{2,10},{4,12},{6,14},{8,0},{10,2},{12,4},{14,6},{16,24},{18,... | collective-permute-start | bytes 3145736 | tf_op jit(solution)/shard_map/ppermute | solution.py:96
  127.3 12.1 %collective-permute-start.14 = (f32[2,2,1,2,1,8,2048]{6,5,4,3,2,1,0:T(8,128)S(1)}, f32[2,2,1,2,1,8,2048]{6,5,4,3,2,1,0:T(8,128)S(1)}, u32[]{:S(2)}, u32[]{:S(2)}) collective-permute-start(f32[2,2,1,2,1,8,2048]{6,5,4,3,2,1,0:T(8,128)S(1)} %slice_select_fusion.3), channel_id=1, source_target_pairs={{0,8},{2,10},{4,12},{6,14},{8,0},{10,2},{12,4},{14,6},{16,24},{18,... | collective-permute-start | bytes 1572872 | tf_op jit(solution)/shard_map/ppermute | solution.py:96
  130.3 10.2 %collective-permute-start.19 = (f32[2,2,1,2,1,8,2048]{6,5,4,3,2,1,0:T(8,128)S(1)}, f32[2,2,1,2,1,8,2048]{6,5,4,3,2,1,0:T(8,128)S(1)}, u32[]{:S(2)}, u32[]{:S(2)}) collective-permute-start(f32[2,2,1,2,1,8,2048]{6,5,4,3,2,1,0:T(8,128)S(1)} %slice_select_fusion.2), channel_id=1, source_target_pairs={{0,2},{2,0},{4,6},{6,4},{8,10},{10,8},{12,14},{14,12},{16,18},{18,... | collective-permute-start | bytes 1572872 | tf_op jit(solution)/shard_map/ppermute | solution.py:96
  139.5 8.4 %collective-permute-start.15 = (f32[2,2,1,1,1,8,2048]{6,5,4,3,2,1,0:T(8,128)S(1)}, f32[2,2,1,1,1,8,2048]{6,5,4,3,2,1,0:T(8,128)S(1)}, u32[]{:S(2)}, u32[]{:S(2)}) collective-permute-start(f32[2,2,1,1,1,8,2048]{6,5,4,3,2,1,0:T(8,128)S(1)} %slice_select_fusion.5), channel_id=1, source_target_pairs={{0,4},{2,6},{4,0},{6,2},{8,12},{10,14},{12,8},{14,10},{16,20},{18,... | collective-permute-start | bytes 786440 | tf_op jit(solution)/shard_map/ppermute | solution.py:96
  140.6 12.5 %collective-permute-start.20 = (f32[2,1,1,2,1,8,2048]{6,5,4,3,2,1,0:T(8,128)S(1)}, f32[2,1,1,2,1,8,2048]{6,5,4,3,2,1,0:T(8,128)S(1)}, u32[]{:S(2)}, u32[]{:S(2)}) collective-permute-start(f32[2,1,1,2,1,8,2048]{6,5,4,3,2,1,0:T(8,128)S(1)} %slice_select_fusion.4), channel_id=1, source_target_pairs={{0,16},{2,18},{4,20},{6,22},{8,24},{10,26},{12,28},{14,30},{16,0},... | collective-permute-start | bytes 786440 | tf_op jit(solution)/shard_map/ppermute | solution.py:96
  148.0 10.5 %collective-permute-start.16 = (f32[2,1,1,1,1,8,2048]{6,5,4,3,2,1,0:T(8,128)S(1)}, f32[2,1,1,1,1,8,2048]{6,5,4,3,2,1,0:T(8,128)S(1)}, u32[]{:S(2)}, u32[]{:S(2)}) collective-permute-start(f32[2,1,1,1,1,8,2048]{6,5,4,3,2,1,0:T(8,128)S(1)} %slice_select_fusion.7), channel_id=1, source_target_pairs={{0,16},{2,18},{4,20},{6,22},{8,24},{10,26},{12,28},{14,30},{16,0},... | collective-permute-start | bytes 393224 | tf_op jit(solution)/shard_map/ppermute | solution.py:96
  153.2 8.3 %collective-permute-start.21 = (f32[2,1,1,1,1,8,2048]{6,5,4,3,2,1,0:T(8,128)S(1)}, f32[2,1,1,1,1,8,2048]{6,5,4,3,2,1,0:T(8,128)S(1)}, u32[]{:S(2)}, u32[]{:S(2)}) collective-permute-start(f32[2,1,1,1,1,8,2048]{6,5,4,3,2,1,0:T(8,128)S(1)} %slice_select_fusion.6), channel_id=1, source_target_pairs={{0,4},{2,6},{4,0},{6,2},{8,12},{10,14},{12,8},{14,10},{16,20},{18,... | collective-permute-start | bytes 393224 | tf_op jit(solution)/shard_map/ppermute | solution.py:96
  158.6 9.1 %collective-permute-start.17 = (f32[1,1,1,1,1,8,2048]{6,5,4,3,2,1,0:T(8,128)S(1)}, f32[1,1,1,1,1,8,2048]{6,5,4,3,2,1,0:T(8,128)S(1)}, u32[]{:S(2)}, u32[]{:S(2)}) collective-permute-start(f32[1,1,1,1,1,8,2048]{6,5,4,3,2,1,0:T(8,128)S(1)} %slice_select_fusion.9), channel_id=1, source_target_pairs={{0,32},{2,34},{4,36},{6,38},{8,40},{10,42},{12,44},{14,46},{16,48}... | collective-permute-start | bytes 196616 | tf_op jit(solution)/shard_map/ppermute | solution.py:96
  161.5 8.3 %collective-permute-start.22 = (f32[1,1,1,1,1,8,2048]{6,5,4,3,2,1,0:T(8,128)S(1)}, f32[1,1,1,1,1,8,2048]{6,5,4,3,2,1,0:T(8,128)S(1)}, u32[]{:S(2)}, u32[]{:S(2)}) collective-permute-start(f32[1,1,1,1,1,8,2048]{6,5,4,3,2,1,0:T(8,128)S(1)} %slice_select_fusion.8), channel_id=1, source_target_pairs={{0,32},{2,34},{4,36},{6,38},{8,40},{10,42},{12,44},{14,46},{16,48}... | collective-permute-start | bytes 196616 | tf_op jit(solution)/shard_map/ppermute | solution.py:96
  190.7 8.0 %collective-permute-start.31 = (bf16[2,1,1,2,1,8,2048]{6,5,4,3,2,1,0:T(8,128)(2,1)S(1)}, bf16[2,1,1,2,1,8,2048]{6,5,4,3,2,1,0:T(8,128)(2,1)S(1)}, u32[]{:S(2)}, u32[]{:S(2)}) collective-permute-start(bf16[2,1,1,2,1,8,2048]{6,5,4,3,2,1,0:T(8,128)(2,1)S(1)} %pad_maximum_fusion.19), channel_id=1, source_target_pairs={{0,16},{2,18},{4,20},{6,22},{8,24},{10,26},{12,28},{14,30},{16,0},... | collective-permute-start | bytes 393224 | tf_op jit(solution)/shard_map/ppermute | solution.py:68
  198.7 9.3 %collective-permute-start.27 = (bf16[2,2,1,2,1,8,2048]{6,5,4,3,2,1,0:T(8,128)(2,1)S(1)}, bf16[2,2,1,2,1,8,2048]{6,5,4,3,2,1,0:T(8,128)(2,1)S(1)}, u32[]{:S(2)}, u32[]{:S(2)}) collective-permute-start(bf16[2,2,1,2,1,8,2048]{6,5,4,3,2,1,0:T(8,128)(2,1)S(1)} %pad_maximum_fusion.14), channel_id=1, source_target_pairs={{0,8},{2,10},{4,12},{6,14},{8,0},{10,2},{12,4},{14,6},{16,24},{18,... | collective-permute-start | bytes 786440 | tf_op jit(solution)/shard_map/ppermute | solution.py:68
  198.8 10.3 %collective-permute-start.32 = (bf16[2,2,1,2,1,8,2048]{6,5,4,3,2,1,0:T(8,128)(2,1)S(1)}, bf16[2,2,1,2,1,8,2048]{6,5,4,3,2,1,0:T(8,128)(2,1)S(1)}, u32[]{:S(2)}, u32[]{:S(2)}) collective-permute-start(bf16[2,2,1,2,1,8,2048]{6,5,4,3,2,1,0:T(8,128)(2,1)S(1)} %pad_maximum_fusion.15), channel_id=1, source_target_pairs={{0,2},{2,0},{4,6},{6,4},{8,10},{10,8},{12,14},{14,12},{16,18},{18,... | collective-permute-start | bytes 786440 | tf_op jit(solution)/shard_map/ppermute | solution.py:68
  208.1 9.3 %collective-permute-start.28 = (bf16[2,2,2,2,1,8,2048]{6,5,4,3,2,1,0:T(8,128)(2,1)S(1)}, bf16[2,2,2,2,1,8,2048]{6,5,4,3,2,1,0:T(8,128)(2,1)S(1)}, u32[]{:S(2)}, u32[]{:S(2)}) collective-permute-start(bf16[2,2,2,2,1,8,2048]{6,5,4,3,2,1,0:T(8,128)(2,1)S(1)} %pad_maximum_fusion.10), channel_id=1, source_target_pairs={{0,2},{2,0},{4,6},{6,4},{8,10},{10,8},{12,14},{14,12},{16,18},{18,... | collective-permute-start | bytes 1572872 | tf_op jit(solution)/shard_map/ppermute | solution.py:68
  209.2 9.3 %collective-permute-start.33 = (bf16[2,2,1,2,2,8,2048]{6,5,4,3,2,1,0:T(8,128)(2,1)S(1)}, bf16[2,2,1,2,2,8,2048]{6,5,4,3,2,1,0:T(8,128)(2,1)S(1)}, u32[]{:S(2)}, u32[]{:S(2)}) collective-permute-start(bf16[2,2,1,2,2,8,2048]{6,5,4,3,2,1,0:T(8,128)(2,1)S(1)} %pad_maximum_fusion.11), channel_id=1, source_target_pairs={{0,8},{2,10},{4,12},{6,14},{8,0},{10,2},{12,4},{14,6},{16,24},{18,... | collective-permute-start | bytes 1572872 | tf_op jit(solution)/shard_map/ppermute | solution.py:68
  (36 other events, 214.8 us)
Sparse Core Ops, SparseCore 0:
  220.4 83.5 all-gather.1
